TPU v7x, 32 devices: a whole 2x2x4 slice. The times are simulated.
32 devices in a mesh: expert: 8 (over z, x), tensor: 4 (over y, core).
Axes of the slice: x: 2, y: 2, z: 4, core: 2. Of those that a mesh axis runs over, the one named last changes fastest.
Arguments:
- context: bfloat16 [2048, 2048], P('expert', 'tensor'), may hold values from -0.25976562 to 0.25976562
- out_proj: bfloat16 [2048, 2048], P('tensor'), may hold values from -0.125 to 0.125
- residual: bfloat16 [2048, 2048], P(('expert', 'tensor')), may hold values from -0.25976562 to 0.25976562
- norm_gain: float32 [2048], replicated, may hold values from 0.1 to 1.9
- router_weight: float32 [2048, 64], replicated, may hold values from -5.524272 to 5.524272
- expert_ids: int32 [2048, 8], P('expert'), may hold values from 0 to 63, all different within a row; in each aligned block of 64 rows (0 to 63, 64 to 127, ...) at most 10 rows name the same one
- placement: int32 [128], replicated, may hold values from 0 to 63, as said below
- expert_weights: bfloat16 [128, 3, 2048, 1024], P('expert', None, None, 'tensor'), as said below
- post_gain: float32 [2048], replicated, may hold values from 0.5 to 1.5
Outputs:
- hidden_out: float32 [2048, 2048], P(('expert', 'tensor'))
- normed_out: float32 [2048, 2048], P(('expert', 'tensor'))
Inputs may be any that keep to these rules, and one draw needn't show every extreme that they name: `expert_ids`: each row names 8 different experts. In each aligned block of 64 rows (the rows of one device) no expert is named by more than 10 rows, a bound that some block reaches; every expert is named somewhere. `placement`: every expert is held by one, three or five slots. `expert_weights`: slots that hold the same expert carry equal weights.
All inputs are finite; a program needn't handle non-finite values.
Results may differ from a plain program's by a relative error of at most 0.018.
Values may be sent and summed in bfloat16 or wider, within the bound.
No kernel may reach another device: no remote copies, remote signals or barrier semaphores. Data moves between devices by JAX's collectives and lax.ppermute only.
A program may use at most 256 MiB of HBM per device.

v0:
```python
import jax
import jax.numpy as jnp
from jax import lax
from jax.sharding import PartitionSpec as P

EPS = 1e-06


def rms_scale(values, gain_row):
    mean_square = jnp.mean(values * values, axis=-1, keepdims=True)
    return values * lax.rsqrt(mean_square + EPS) * gain_row


def expert_partial(block_rows, weights):
    gate_pre = jnp.einsum(
        "nqsmd,sdf->nqsmf", block_rows, weights[:, 0], preferred_element_type=jnp.float32
    )
    up_pre = jnp.einsum(
        "nqsmd,sdf->nqsmf", block_rows, weights[:, 1], preferred_element_type=jnp.float32
    )
    inner_act = (jax.nn.silu(gate_pre) * up_pre).astype(jnp.bfloat16)
    return jnp.einsum(
        "nqsmf,sdf->nqsmd", inner_act, weights[:, 2], preferred_element_type=jnp.float32
    )


def on_device(
    context,
    out_proj,
    residual,
    norm_gain,
    router_weight,
    expert_ids,
    placement,
    expert_weights,
    post_gain,
):
    groups = lax.axis_size("tensor")
    holders = lax.axis_size("expert")
    my_group = lax.axis_index("tensor")
    my_holder = lax.axis_index("expert")
    row_count = residual.shape[0]
    model_width = residual.shape[1]
    top_count = expert_ids.shape[1]
    expert_count = router_weight.shape[1]
    slot_dev = expert_weights.shape[0]
    slot_total = placement.shape[0]
    capacity = max(2, row_count * top_count * 5 // (expert_count * 4))
    expert_range = jnp.arange(expert_count, dtype=jnp.int32)
    slot_range = jnp.arange(slot_total, dtype=jnp.int32)
    attention = lax.psum_scatter(
        jnp.dot(context, out_proj, preferred_element_type=jnp.float32).astype(jnp.bfloat16),
        "tensor",
        scatter_dimension=0,
        tiled=True,
    ).astype(jnp.float32)
    hidden_mid = residual.astype(jnp.float32) + attention
    normed_full = rms_scale(hidden_mid, norm_gain)
    normed = normed_full.astype(jnp.bfloat16)
    logits = jnp.dot(normed_full, router_weight, precision=lax.Precision.HIGHEST)
    own_ids = lax.dynamic_slice_in_dim(expert_ids, my_group * row_count, row_count, 0)
    own_onehot = own_ids[:, :, None] == expert_range[None, None, :]
    chosen = jnp.sum(jnp.where(own_onehot, logits[:, None, :], 0.0), axis=-1)
    gate_weights = jax.nn.softmax(chosen, axis=-1)
    holds = (placement[None, :] == expert_range[:, None]).astype(jnp.int32)
    copies = jnp.sum(holds, axis=1)
    copy_rank = jnp.cumsum(holds, axis=1) - 1
    copy_pick = my_holder % copies
    picked = (holds > 0) & (copy_rank == copy_pick[:, None])
    slot_pick = jnp.sum(jnp.where(picked, slot_range[None, :], 0), axis=1)
    group_rows = lax.all_gather(normed, "tensor", axis=0, tiled=True)
    ids_block = expert_ids.reshape(groups, row_count, top_count)
    quarters = ids_block.shape[0]
    flat_ids = ids_block.reshape(quarters, -1)
    onehot = flat_ids[:, :, None] == expert_range
    slot_of = jnp.sum(jnp.where(onehot, slot_pick, 0), axis=-1)
    slot_hot = (slot_of[:, :, None] == slot_range).astype(jnp.int32)
    rank_in = jnp.sum(jnp.cumsum(slot_hot, axis=1) * slot_hot, axis=-1) - 1
    holder_all = slot_of // slot_dev
    local_all = slot_of % slot_dev
    rank_all = rank_in
    quarters = holder_all.shape[0]
    quarter_ids = jnp.arange(quarters, dtype=jnp.int32)[:, None]
    target = (
        ((holder_all * quarters + quarter_ids) * slot_dev + local_all) * capacity + rank_all
    ).reshape(-1)
    source_rows = jnp.repeat(group_rows, top_count, axis=0)
    send_buffer = jnp.zeros((holders * quarters * slot_dev * capacity, model_width), jnp.bfloat16)
    send_buffer = send_buffer.at[target].set(source_rows, unique_indices=True)
    send_buffer = send_buffer.reshape(holders, quarters, slot_dev, capacity, model_width)
    received = lax.all_to_all(send_buffer, "expert", split_axis=0, concat_axis=0, tiled=True)
    holder = lax.dynamic_index_in_dim(holder_all, my_group, 0, keepdims=False)
    local_slot = lax.dynamic_index_in_dim(local_all, my_group, 0, keepdims=False)
    rank_in = lax.dynamic_index_in_dim(rank_all, my_group, 0, keepdims=False)
    partial_value = expert_partial(received, expert_weights)
    expert_sum = lax.psum_scatter(
        partial_value.astype(jnp.bfloat16), "tensor", scatter_dimension=1, tiled=True
    )
    returned = lax.all_to_all(expert_sum, "expert", split_axis=0, concat_axis=0, tiled=True)
    own_index = (holder * slot_dev + local_slot) * capacity + rank_in
    outputs = returned.reshape(-1, model_width)[own_index].reshape(
        row_count, top_count, model_width
    )
    moe_sum = jnp.einsum("rk,rkd->rd", gate_weights, outputs.astype(jnp.float32))
    hidden_out = hidden_mid + moe_sum
    normed_out = rms_scale(hidden_out, post_gain)
    return (hidden_out, normed_out)


def solution(mesh):
    in_specs = (
        P("expert", "tensor"),
        P("tensor", None),
        P(("expert", "tensor"), None),
        P(),
        P(),
        P("expert", None),
        P(),
        P("expert", None, None, "tensor"),
        P(),
    )
    out_specs = (P(("expert", "tensor"), None), P(("expert", "tensor"), None))
    return jax.shard_map(
        on_device, mesh=mesh, in_specs=in_specs, out_specs=out_specs, check_vma=False
    )
```

profile of v0, /device:TPU:0, one launch (start us, length us, event | category | flops | bytes accessed | tf_op | source)
XLA Modules:
  0.0 1007.2 jit_solution(1914722474979236487)
XLA Ops:
  7.2 1.5 copy-done
  8.8 2.7 convolution_convert_fusion
  11.5 0.8 copy.53
  12.4 0.7 fusion.37
  13.1 0.3 reduce_window_sum.26
  13.4 0.8 fusion.39
  14.3 0.8 select_reduce_fusion.2
  15.5 23.7 %reduce-scatter.3.cloned.1.call-done = bf16[64,2048]{1,0:T(8,128)(2,1)} async-done(((bf16[256,2048]{1,0:T(8,128)(2,1)}), bf16[64,2048]{1,0:T(8,128)(2,1)}) %reduce-scatter.3.cloned.1.call-update) | async-done | bytes 262160 | tf_op jit(solution)/shard_map/reduce_scatter | solution.py:51
  39.2 1.2 multiply_reduce_fusion.1
  40.4 1.9 fusion.33
  42.3 0.9 fusion.30
  43.6 0.6 fusion.29
  44.4 14.8 %all-gather.2.cloned.1.call-done = bf16[256,2048]{1,0:T(8,128)(2,1)} async-done(((bf16[64,2048]{1,0:T(8,128)(2,1)}), bf16[256,2048]{1,0:T(8,128)(2,1)}) %all-gather.2.cloned.1.call-update) | async-done | bytes 1048592 | tf_op jit(solution)/shard_map/all_gather | solution.py:71
  59.2 24.1 %scatter_custom_fusion = bf16[5120,2048]{1,0:T(8,128)(2,1)} fusion(s32[2048]{0:T(1024)S(1)} %bitcast.121, bf16[]{:T(256)} %constant.84.clone.1, bf16[256,2048]{1,0:T(8,128)(2,1)} %all-gather.2.cloned.1.call-done), kind=kCustom, calls=%fused_computation.13 | custom fusion | bytes 22020098 | tf_op jit(solution)/shard_map/scatter | solution.py:89
  83.3 34.0 %reshape.258 = bf16[8,4,16,10,2048]{4,3,2,1,0:T(8,128)(2,1)} reshape(bf16[5120,2048]{1,0:T(8,128)(2,1)} %scatter_custom_fusion) | data formatting | bytes 41943040 | tf_op jit(solution)/shard_map/reshape | solution.py:90
  117.3 19.2 %copy.56 = bf16[8,4,16,10,2048]{4,2,3,1,0:T(8,128)(2,1)S(1)} copy(bf16[8,4,16,10,2048]{4,3,2,1,0:T(8,128)(2,1)} %reshape.258) | data formatting | bytes 41943040 | tf_op jit(solution)/shard_map/reshape | solution.py:90
  136.5 458.7 %all_to_all.10 = bf16[8,4,16,10,2048]{4,2,3,1,0:T(8,128)(2,1)} all-to-all(bf16[8,4,16,10,2048]{4,2,3,1,0:T(8,128)(2,1)S(1)} %copy.56), channel_id=1, replica_groups=mesh['expert'=8,'tensor'=4] {'expert'}, dimensions={0} | all-to-all | bytes 41943040 | tf_op jit(solution)/shard_map/all_to_all | solution.py:91
  595.2 27.0 %fusion = f32[16,8,4,10,256]{4,3,2,1,0:T(8,128)} fusion(bf16[8,4,16,10,2048]{4,2,3,1,0:T(8,128)(2,1)} %all_to_all.10, bf16[16,3,2048,256]{3,2,1,0:T(8,128)(2,1)} %param.16), kind=kOutput, calls=%fused_computation.2 | convolution fusion | flops 5368709120 | bytes 42991616 | tf_op jit(solution)/shard_map/nqsmd,sdf->nqsmf/dot_general | solution.py:18
  622.2 27.7 %fusion.12.clone.5 = bf16[8,4,16,10,256]{4,3,1,0,2:T(8,128)(2,1)} fusion(f32[16,8,4,10,256]{4,3,2,1,0:T(8,128)} %fusion, bf16[16,3,2048,256]{3,2,1,0:T(8,128)(2,1)} %param.16, bf16[8,4,16,10,2048]{4,2,3,1,0:T(8,128)(2,1)} %all_to_all.10), kind=kOutput, calls=%fused_computation.16.clone.clone.clone.2 | convolution fusion | flops 5376573440 | bytes 48758784 | tf_op jit(solution)/shard_map/nqsmd,sdf->nqsmf/dot_general | solution.py:15
  649.9 21.4 %convert_bitcast_fusion = bf16[8,4,16,10,2048]{4,3,1,0,2:T(8,128)(2,1)} fusion(bf16[16,3,2048,256]{3,2,1,0:T(8,128)(2,1)} %param.16, bf16[8,4,16,10,256]{4,3,1,0,2:T(8,128)(2,1)} %fusion.12.clone.5), kind=kOutput, calls=%fused_computation.6 | convolution fusion | flops 5379194880 | bytes 41943040 | tf_op jit(solution)/shard_map/nqsmf,sdf->nqsmd/dot_general | solution.py:22
  671.4 24.4 %copy.62 = bf16[8,4,16,10,2048]{4,2,3,0,1:T(8,128)(2,1)} copy(bf16[8,4,16,10,2048]{4,3,1,0,2:T(8,128)(2,1)} %convert_bitcast_fusion) | data formatting | bytes 41943040 | tf_op jit(solution)/shard_map/convert_element_type | solution.py:97
  695.8 151.3 %reduce-scatter.5.cloned.1.call-done = bf16[8,1,16,10,2048]{4,2,3,0,1:T(8,128)(2,1)} async-done(((bf16[8,4,16,10,2048]{4,2,3,0,1:T(8,128)(2,1)}), bf16[8,1,16,10,2048]{4,2,3,0,1:T(8,128)(2,1)}) %reduce-scatter.5.cloned.1.call-update) | async-done | bytes 5242896 | tf_op jit(solution)/shard_map/reduce_scatter | solution.py:96
  847.2 5.5 all-to-all-start.1
  852.9 0.7 fusion.34
  853.6 0.2 select_reduce_fusion.1
  854.2 114.3 %all-to-all-done.1 = bf16[8,1,16,10,2048]{4,2,3,1,0:T(8,128)(2,1)} async-done(((bf16[8,1,16,10,2048]{4,2,3,1,0:T(8,128)(2,1)}), bf16[8,1,16,10,2048]{4,2,3,1,0:T(8,128)(2,1)}, u32[]{:S(2)}, u32[]{:S(2)}) %all-to-all-start.1) | async-done | bytes 5242912 | tf_op jit(solution)/shard_map/all_to_all | solution.py:99
  968.4 9.7 copy.64
  978.2 10.0 reshape.259
  988.2 8.5 gather_fusion
  996.6 2.3 fusion.27
  998.9 0.3 multiply_reduce_fusion
  999.2 0.9 multiply_multiply_fusion
  (51 shorter events, 1.8 us)
Async XLA Ops:
  7.2 1.6 copy-start
  7.2 32.0 %reduce-scatter.3.cloned.1.call-start = ((), (), s32[]{:S(2)}) async-start(), calls=%async_computation.4 | async-start | bytes 1310720 | tf_op jit(solution)/shard_map/reduce_scatter | solution.py:51
  11.4 47.7 %all-gather.2.cloned.1.call-start = ((), (), s32[]{:S(2)}) async-start(), calls=%async_computation.5 | async-start | bytes 1310720 | tf_op jit(solution)/shard_map/all_gather | solution.py:71
  42.3 804.9 %reduce-scatter.5.cloned.1.call-start = ((), (), s32[]{:S(2)}) async-start(), calls=%async_computation.6 | async-start | bytes 26214400 | tf_op jit(solution)/shard_map/reduce_scatter | solution.py:96
  695.8 156.9 %copy-start.7 = (s32[256,8]{0,1:T(8,128)S(1)}, s32[256,8]{0,1:T(8,128)}, u32[]{:S(2)}) copy-start(s32[256,8]{0,1:T(8,128)} %param.14) | copy-start | bytes 24580
  695.8 157.1 %copy-start.2 = (bf16[64,2048]{1,0:T(8,128)(2,1)S(1)}, bf16[64,2048]{1,0:T(8,128)(2,1)}, u32[]{:S(2)}) copy-start(bf16[64,2048]{1,0:T(8,128)(2,1)} %param.11) | copy-start | bytes 786436
  695.8 157.1 %copy-start.3 = (bf16[64,2048]{1,0:T(8,128)(2,1)S(1)}, bf16[64,2048]{1,0:T(8,128)(2,1)}, u32[]{:S(2)}) copy-start(bf16[64,2048]{1,0:T(8,128)(2,1)} %reduce-scatter.3.cloned.1.call-done) | copy-start | bytes 786436
  695.8 157.1 %copy-start.5 = (f32[2048,64]{0,1:T(8,128)S(1)}, f32[2048,64]{0,1:T(8,128)}, u32[]{:S(2)}) copy-start(f32[2048,64]{0,1:T(8,128)} %param.13) | copy-start | bytes 1572868
  695.8 157.1 %copy-start.6 = (f32[2048]{0:T(1024)S(1)}, f32[2048]{0:T(1024)}, u32[]{:S(2)}) copy-start(f32[2048]{0:T(1024)} %param.12) | copy-start | bytes 24580
  847.2 121.3 %all-to-all-start.1 = ((bf16[8,1,16,10,2048]{4,2,3,1,0:T(8,128)(2,1)}), bf16[8,1,16,10,2048]{4,2,3,1,0:T(8,128)(2,1)}, u32[]{:S(2)}, u32[]{:S(2)}) async-start(bf16[8,1,16,10,2048]{4,2,3,1,0:T(8,128)(2,1)} %bitcast.116), calls=%async_computation.3 | async-start | bytes 10485760 | tf_op jit(solution)/shard_map/all_to_all | solution.py:99
  978.2 22.0 %copy-start.1 = (bf16[512,2048]{1,0:T(8,128)(2,1)S(1)}, bf16[512,2048]{1,0:T(8,128)(2,1)}, u32[]{:S(2)}) copy-start(bf16[512,2048]{1,0:T(8,128)(2,1)} %param.10) | copy-start | bytes 6291460
  988.2 11.1 %copy-start.8 = (f32[2048]{0:T(1024)S(1)}, f32[2048]{0:T(1024)}, u32[]{:S(2)}) copy-start(f32[2048]{0:T(1024)} %param.17) | copy-start | bytes 24580
  999.2 1.0 copy-start.4
Sparse Core Ops, SparseCore 0:
  11.6 27.5 reduce-scatter.2
  42.4 16.7 all-gather.1
  695.9 151.2 reduce-scatter.4
where the time goes:
time: 1020 us; the launch traced here: 1010 us
  blocking collectives  459 us (45%)
  waiting for transfers between devices  304 us (30%)
  local copies, waits for them, and re-layouts  133 us (13%)
  matrix products  81.7 us (8%)
  between operations  14.5 us (1%)
    all_to_all x1, blocking collectives, on_device(): lax.all_to_all(send_buffer, 'expert', split_axis=0, concat_axis=0, tiled=...  459 us
    reduce_scatter x1, waiting for transfers between devices, on_device(): lax.psum_scatter(partial_value.astype(jnp.bfloat16), 'tensor', scatter_di...  151 us
    all_to_all x1, waiting for transfers between devices, on_device(): lax.all_to_all(expert_sum, 'expert', split_axis=0, concat_axis=0, tiled=T...  114 us
    reshape x2, local copies, waits for them, and re-layouts, on_device(): send_buffer.reshape(holders, quarters, slot_dev, capacity, model_width)  53.2 us
    dot_general x1, matrix products, expert_partial(): jnp.einsum('nqsmd,sdf->nqsmf', block_rows, weights[:, 0], preferred_eleme...  27.7 us
    dot_general x1, matrix products, expert_partial(): jnp.einsum('nqsmd,sdf->nqsmf', block_rows, weights[:, 1], preferred_eleme...  27 us
    convert_element_type x1, local copies, waits for them, and re-layouts, on_device(): partial_value.astype(jnp.bfloat16)  24.4 us
    scatter x1, local copies, waits for them, and re-layouts, on_device(): send_buffer = send_buffer.at[target].set(source_rows, unique_indices=True)  24.1 us
  transfers between devices with their start and end apart: 4, of which 4 were waited for; matrix products, arithmetic and copies ran while one was open for 1% of the time, Pallas kernels for 0%

commit v1 on v0

--- a/solution.py
+++ b/solution.py
@@ -45,6 +45,7 @@
     expert_count = router_weight.shape[1]
     slot_dev = expert_weights.shape[0]
     slot_total = placement.shape[0]
+    blocks = holders * groups
     capacity = max(2, row_count * top_count * 5 // (expert_count * 4))
     expert_range = jnp.arange(expert_count, dtype=jnp.int32)
     slot_range = jnp.arange(slot_total, dtype=jnp.int32)
@@ -62,36 +63,39 @@
     own_onehot = own_ids[:, :, None] == expert_range[None, None, :]
     chosen = jnp.sum(jnp.where(own_onehot, logits[:, None, :], 0.0), axis=-1)
     gate_weights = jax.nn.softmax(chosen, axis=-1)
+    all_rows = lax.all_gather(normed, ("expert", "tensor"), axis=0, tiled=True)
+    all_ids = lax.all_gather(expert_ids, "expert", axis=0, tiled=True)
     holds = (placement[None, :] == expert_range[:, None]).astype(jnp.int32)
     copies = jnp.sum(holds, axis=1)
     copy_rank = jnp.cumsum(holds, axis=1) - 1
-    copy_pick = my_holder % copies
-    picked = (holds > 0) & (copy_rank == copy_pick[:, None])
-    slot_pick = jnp.sum(jnp.where(picked, slot_range[None, :], 0), axis=1)
-    group_rows = lax.all_gather(normed, "tensor", axis=0, tiled=True)
-    ids_block = expert_ids.reshape(groups, row_count, top_count)
-    quarters = ids_block.shape[0]
-    flat_ids = ids_block.reshape(quarters, -1)
+    holder_range = jnp.arange(holders, dtype=jnp.int32)
+    copy_pick = holder_range[:, None] % copies[None, :]
+    picked = (holds[None] > 0) & (copy_rank[None] == copy_pick[:, :, None])
+    slot_pick = jnp.sum(jnp.where(picked, slot_range[None, None, :], 0), axis=2)
+    flat_ids = all_ids.reshape(blocks, row_count * top_count)
+    block_holder = jnp.arange(blocks, dtype=jnp.int32) // groups
+    block_pick = slot_pick[block_holder]
     onehot = flat_ids[:, :, None] == expert_range
-    slot_of = jnp.sum(jnp.where(onehot, slot_pick, 0), axis=-1)
+    slot_of = jnp.sum(jnp.where(onehot, block_pick[:, None, :], 0), axis=-1)
     slot_hot = (slot_of[:, :, None] == slot_range).astype(jnp.int32)
-    rank_in = jnp.sum(jnp.cumsum(slot_hot, axis=1) * slot_hot, axis=-1) - 1
+    rank_all = jnp.sum(jnp.cumsum(slot_hot, axis=1) * slot_hot, axis=-1) - 1
     holder_all = slot_of // slot_dev
     local_all = slot_of % slot_dev
-    rank_all = rank_in
-    quarters = holder_all.shape[0]
-    quarter_ids = jnp.arange(quarters, dtype=jnp.int32)[:, None]
-    target = (
-        ((holder_all * quarters + quarter_ids) * slot_dev + local_all) * capacity + rank_all
-    ).reshape(-1)
-    source_rows = jnp.repeat(group_rows, top_count, axis=0)
-    send_buffer = jnp.zeros((holders * quarters * slot_dev * capacity, model_width), jnp.bfloat16)
-    send_buffer = send_buffer.at[target].set(source_rows, unique_indices=True)
-    send_buffer = send_buffer.reshape(holders, quarters, slot_dev, capacity, model_width)
-    received = lax.all_to_all(send_buffer, "expert", split_axis=0, concat_axis=0, tiled=True)
-    holder = lax.dynamic_index_in_dim(holder_all, my_group, 0, keepdims=False)
-    local_slot = lax.dynamic_index_in_dim(local_all, my_group, 0, keepdims=False)
-    rank_in = lax.dynamic_index_in_dim(rank_all, my_group, 0, keepdims=False)
+    block_ids = jnp.arange(blocks, dtype=jnp.int32)[:, None]
+    token_of = block_ids * row_count + jnp.arange(row_count * top_count, dtype=jnp.int32)[None, :] // top_count
+    mine = holder_all == my_holder
+    row_total = blocks * slot_dev * capacity
+    target = jnp.where(mine, (block_ids * slot_dev + local_all) * capacity + rank_all, row_total)
+    index_table = jnp.zeros((row_total,), jnp.int32).at[target.reshape(-1)].set(
+        token_of.reshape(-1), mode="drop", unique_indices=True
+    )
+    received = jnp.take(all_rows, index_table, axis=0).reshape(
+        holders, groups, slot_dev, capacity, model_width
+    )
+    own_block = my_holder * groups + my_group
+    holder = lax.dynamic_index_in_dim(holder_all, own_block, 0, keepdims=False)
+    local_slot = lax.dynamic_index_in_dim(local_all, own_block, 0, keepdims=False)
+    rank_in = lax.dynamic_index_in_dim(rank_all, own_block, 0, keepdims=False)
     partial_value = expert_partial(received, expert_weights)
     expert_sum = lax.psum_scatter(
         partial_value.astype(jnp.bfloat16), "tensor", scatter_dimension=1, tiled=True

time: 1020 us -> 631 us (0.62); the launches traced: 1010 us -> 629 us
  blocking collectives: 459 us -> 30.9 us
  local copies, waits for them, and re-layouts: 133 us -> 194 us
  matrix products: 81.7 us -> 65.5 us
  other arithmetic: 9.45 us -> 23.8 us
    all_to_all x1 -> x0, blocking collectives: 459 us -> none  [on_device(): lax.all_to_all(send_buffer, 'expert', split_axis=0, concat_axis=0, tiled=...]
    gather x0 -> x3, local copies, waits for them, and re-layouts: none -> 77.9 us  [the longest x2 77.3 us: on_device(): jnp.take(all_rows, index_table, axis=0)]
    reshape x2 -> x0, local copies, waits for them, and re-layouts: 53.2 us -> none  [on_device(): send_buffer.reshape(holders, quarters, slot_dev, capacity, model_width)]
    scatter x1, local copies, waits for them, and re-layouts: 24.1 us -> 60.5 us  [on_device(): jnp.zeros((row_total,), jnp.int32).at[target.reshape(-1)]]
    all_gather x0 -> x1, blocking collectives: none -> 30.9 us  [on_device(): all_ids = lax.all_gather(expert_ids, 'expert', axis=0, tiled=True)]
    dot_general x1 -> x0, matrix products: 27.7 us -> none  [expert_partial(): jnp.einsum('nqsmd,sdf->nqsmf', block_rows, weights[:, 0], preferred_eleme...]
    dot_general x1, matrix products: 21.4 us -> 39.2 us  [expert_partial(): jnp.einsum('nqsmf,sdf->nqsmd', inner_act, weights[:, 2], preferred_elemen...]
    all_gather x1, waiting for transfers between devices: 14.8 us -> 0.02 us  [on_device(): all_rows = lax.all_gather(normed, ('expert', 'tensor'), axis=0, tiled=True)]
  transfers between devices with their start and end apart: 4 -> 4, of which waited for: 4 -> 3; matrix products, arithmetic and copies ran while one was open for 1% -> 13% of each run, Pallas kernels for 0% -> 0%
where the time goes in v1:
time: 631 us; the launch traced here: 629 us
  waiting for transfers between devices  294 us (47%)
  local copies, waits for them, and re-layouts  194 us (31%)
  matrix products  65.5 us (10%)
  blocking collectives  30.9 us (5%)
  other arithmetic  23.8 us (4%)
  between operations  14.2 us (2%)
    reduce_scatter x1, waiting for transfers between devices, on_device(): lax.psum_scatter(partial_value.astype(jnp.bfloat16), 'tensor', scatter_di...  153 us
    all_to_all x1, waiting for transfers between devices, on_device(): lax.all_to_all(expert_sum, 'expert', split_axis=0, concat_axis=0, tiled=T...  113 us
    gather x2, local copies, waits for them, and re-layouts, on_device(): jnp.take(all_rows, index_table, axis=0)  77.3 us
    scatter x1, local copies, waits for them, and re-layouts, on_device(): jnp.zeros((row_total,), jnp.int32).at[target.reshape(-1)]  60.5 us
    dot_general x1, matrix products, expert_partial(): jnp.einsum('nqsmf,sdf->nqsmd', inner_act, weights[:, 2], preferred_elemen...  39.2 us
    all_gather x1, blocking collectives, on_device(): all_ids = lax.all_gather(expert_ids, 'expert', axis=0, tiled=True)  30.9 us
    reduce_scatter x1, waiting for transfers between devices, on_device(): lax.psum_scatter(jnp.dot(context, out_proj, preferred_element_type=jnp.fl...  27.7 us
    convert_element_type x1, local copies, waits for them, and re-layouts, on_device(): partial_value.astype(jnp.bfloat16)  24.3 us
  transfers between devices with their start and end apart: 4, of which 3 were waited for; matrix products, arithmetic and copies ran while one was open for 13% of the time, Pallas kernels for 0%

profile of v1, /device:TPU:0, one launch (start us, length us, event | category | flops | bytes accessed | tf_op | source)
XLA Modules:
  0.0 628.9 jit_solution(16265701694805310592)
XLA Ops:
  7.2 1.5 copy-done
  8.8 2.7 convolution_convert_fusion
  11.5 27.7 %reduce-scatter.3.cloned.1.call-done = bf16[64,2048]{1,0:T(8,128)(2,1)} async-done(((bf16[256,2048]{1,0:T(8,128)(2,1)}), bf16[64,2048]{1,0:T(8,128)(2,1)}) %reduce-scatter.3.cloned.1.call-update) | async-done | bytes 262160 | tf_op jit(solution)/shard_map/reduce_scatter | solution.py:52
  39.2 1.2 multiply_reduce_fusion.1
  40.4 1.8 fusion.29
  42.6 30.9 %all_gather.6 = s32[2048,8]{0,1:T(8,128)S(1)} all-gather(s32[256,8]{0,1:T(8,128)} %param.14), channel_id=1, replica_groups=mesh['expert'=8,'tensor'=4] {'expert'}, dimensions={0}, use_global_device_ids=true | all-gather | bytes 73728 | tf_op jit(solution)/shard_map/all_gather | solution.py:67
  73.5 0.3 copy.65
  73.8 0.5 eq.116
  75.0 0.3 select_reduce_fusion.2
  75.3 0.6 gather_fusion
  75.9 0.8 select_reduce_fusion.1
  76.9 2.5 fusion.14
  79.4 1.1 broadcast_add_fusion
  80.5 11.7 %select_reduce_fusion = s32[32,512]{0,1:T(8,128)S(1)} fusion(s32[32,512,128]{2,0,1:T(8,128)S(1)} %bitcast.112, s32[32,512]{0,1:T(8,128)S(1)} %copy.66), kind=kLoop, calls=%fused_computation.23 | loop fusion | flops 6275072 | bytes 8519680 | tf_op jit(solution)/shard_map/reduce_sum | solution.py:81
  92.3 0.7 broadcast_add_fusion.1
  93.0 0.6 compare_select_fusion
  93.6 60.5 %scatter_custom_fusion = s32[5120]{0:T(1024)S(1)} fusion(s32[16384]{0:T(1024)S(1)} %bitcast.120, s32[16384]{0:T(1024)S(1)} %bitcast.119, s32[]{:T(128)} %constant.121.clone.1), kind=kCustom, calls=%fused_computation.75 | custom fusion | bytes 20484 | tf_op jit(solution)/shard_map/scatter | solution.py:89
  154.5 43.3 %gather_fusion.1 = bf16[5120,2048]{1,0:T(8,128)(2,1)} fusion(bf16[2048,2048]{1,0:T(8,128)(2,1)} %all-gather.2.cloned.1.call-done, s32[5120]{0:T(1024)S(1)} %fusion.38), kind=kCustom, calls=%fused_computation.1 | custom fusion | bytes 41963520 | tf_op jit(solution)/shard_map/jit(_take)/gather | solution.py:92
  197.8 34.0 %gather.14 = bf16[8,4,16,10,2048]{4,3,2,1,0:T(8,128)(2,1)} reshape(bf16[5120,2048]{1,0:T(8,128)(2,1)} %gather_fusion.1) | data formatting | bytes 41943040 | tf_op jit(solution)/shard_map/jit(_take)/gather | solution.py:92
  231.8 20.7 %fusion = f32[16,8,4,10,256]{4,3,2,1,0:T(8,128)} fusion(bf16[16,3,2048,256]{3,2,1,0:T(8,128)(2,1)} %param.16, bf16[8,4,16,10,2048]{4,3,2,1,0:T(8,128)(2,1)} %gather.14, pred[8,4,16,10]{3,2,1,0:T(8,128)(4,1)S(1)} %broadcast_in_dim.96), kind=kOutput, calls=%fused_computation.6 | convolution fusion | flops 5379194880 | bytes 55579648 | tf_op jit(solution)/shard_map/nqsmd,sdf->nqsmf/dot_general | solution.py:18
  252.5 39.2 %convert_bitcast_fusion = bf16[8,4,16,10,2048]{4,3,1,0,2:T(8,128)(2,1)} fusion(bf16[16,3,2048,256]{3,2,1,0:T(8,128)(2,1)} %param.16, f32[16,8,4,10,256]{4,3,2,1,0:T(8,128)} %fusion, bf16[8,4,16,10,2048]{4,3,2,1,0:T(8,128)(2,1)} %gather.14, pred[8,4,16,10]{3,2,1,0:T(8,128)(4,1)S(1)} %broadcast_in_dim.96), kind=kOutput, calls=%fused_computation.4 | convolution fusion | flops 10766254080 | bytes 96474112 | tf_op jit(solution)/shard_map/nqsmf,sdf->nqsmd/dot_general | solution.py:22
  291.7 24.3 %copy.74 = bf16[8,4,16,10,2048]{4,2,3,0,1:T(8,128)(2,1)} copy(bf16[8,4,16,10,2048]{4,3,1,0,2:T(8,128)(2,1)} %convert_bitcast_fusion) | data formatting | bytes 41943040 | tf_op jit(solution)/shard_map/convert_element_type | solution.py:101
  316.1 153.2 %reduce-scatter.5.cloned.1.call-done = bf16[8,1,16,10,2048]{4,2,3,0,1:T(8,128)(2,1)} async-done(((bf16[8,4,16,10,2048]{4,2,3,0,1:T(8,128)(2,1)}), bf16[8,1,16,10,2048]{4,2,3,0,1:T(8,128)(2,1)}) %reduce-scatter.5.cloned.1.call-update) | async-done | bytes 5242896 | tf_op jit(solution)/shard_map/reduce_scatter | solution.py:100
  469.3 5.5 all-to-all-start
  475.1 0.8 compare_select_fusion.6
  475.9 0.7 fusion.30
  477.1 113.5 %all-to-all-done = bf16[8,1,16,10,2048]{4,2,3,1,0:T(8,128)(2,1)} async-done(((bf16[8,1,16,10,2048]{4,2,3,1,0:T(8,128)(2,1)}), bf16[8,1,16,10,2048]{4,2,3,1,0:T(8,128)(2,1)}, u32[]{:S(2)}, u32[]{:S(2)}) %all-to-all-start) | async-done | bytes 5242912 | tf_op jit(solution)/shard_map/all_to_all | solution.py:103
  590.6 9.7 %copy.76 = bf16[8,1,16,10,2048]{4,3,2,0,1:T(8,128)(2,1)} copy(bf16[8,1,16,10,2048]{4,2,3,1,0:T(8,128)(2,1)} %all-to-all-done) | data formatting | bytes 10485760 | tf_op jit(solution)/shard_map/all_to_all | solution.py:103
  600.3 10.0 %reshape.449 = bf16[1280,2048]{1,0:T(8,128)(2,1)} reshape(bf16[8,1,16,10,2048]{4,3,2,0,1:T(8,128)(2,1)} %copy.76) | data formatting | bytes 10485760 | tf_op jit(solution)/shard_map/reshape | solution.py:105
  610.3 8.5 %gather_fusion.2 = bf16[512,2048]{1,0:T(8,128)(2,1)} fusion(bf16[1280,2048]{1,0:T(8,128)(2,1)} %reshape.449, s32[1024]{0:T(1024)S(1)} %pad_clamp_fusion), kind=kCustom, calls=%fused_computation.2 | custom fusion | bytes 4196352 | tf_op jit(solution)/shard_map/gather | solution.py:105
  618.8 2.3 fusion.27
  621.4 0.9 multiply_multiply_fusion
  (72 shorter events, 2.8 us)
Async XLA Ops:
  7.2 1.6 copy-start
  7.2 67.2 %copy-start.13 = (s32[128]{0:T(128)S(1)}, s32[128]{0:T(128)}, u32[]{:S(2)}) copy-start(s32[128]{0:T(128)} %param.15) | copy-start | bytes 1540
  7.2 32.0 %reduce-scatter.3.cloned.1.call-start = ((), (), s32[]{:S(2)}) async-start(), calls=%async_computation.3 | async-start | bytes 1310720 | tf_op jit(solution)/shard_map/reduce_scatter | solution.py:52
  11.4 143.0 %all-gather.2.cloned.1.call-start = ((), (), s32[]{:S(2)}) async-start(), calls=%async_computation.4 | async-start | bytes 8650752 | tf_op jit(solution)/shard_map/all_gather | solution.py:66
  40.4 2.0 copy-start.11
  42.3 427.0 %reduce-scatter.5.cloned.1.call-start = ((), (), s32[]{:S(2)}) async-start(), calls=%async_computation.5 | async-start | bytes 26214400 | tf_op jit(solution)/shard_map/reduce_scatter | solution.py:100
  76.7 3.8 copy-start.5
  316.0 158.8 %copy-start.9 = (s32[256,8]{0,1:T(8,128)S(1)}, s32[256,8]{0,1:T(8,128)}, u32[]{:S(2)}) copy-start(s32[256,8]{0,1:T(8,128)} %param.14) | copy-start | bytes 24580
  316.0 159.0 %copy-start.6 = (s32[32,512]{1,0:T(8,128)S(1)}, s32[32,512]{1,0:T(8,128)}, u32[]{:S(2)}) copy-start(s32[32,512]{1,0:T(8,128)} %copy-done.5) | copy-start | bytes 196612
  316.1 159.8 %copy-start.2 = (bf16[64,2048]{1,0:T(8,128)(2,1)S(1)}, bf16[64,2048]{1,0:T(8,128)(2,1)}, u32[]{:S(2)}) copy-start(bf16[64,2048]{1,0:T(8,128)(2,1)} %param.11) | copy-start | bytes 786436
  316.1 159.8 %copy-start.3 = (bf16[64,2048]{1,0:T(8,128)(2,1)S(1)}, bf16[64,2048]{1,0:T(8,128)(2,1)}, u32[]{:S(2)}) copy-start(bf16[64,2048]{1,0:T(8,128)(2,1)} %reduce-scatter.3.cloned.1.call-done) | copy-start | bytes 786436
  316.1 159.8 %copy-start.7 = (f32[2048,64]{0,1:T(8,128)S(1)}, f32[2048,64]{0,1:T(8,128)}, u32[]{:S(2)}) copy-start(f32[2048,64]{0,1:T(8,128)} %param.13) | copy-start | bytes 1572868
  316.1 159.8 %copy-start.8 = (f32[2048]{0:T(1024)S(1)}, f32[2048]{0:T(1024)}, u32[]{:S(2)}) copy-start(f32[2048]{0:T(1024)} %param.12) | copy-start | bytes 24580
  316.1 159.8 %copy-start.12 = (f32[64]{0:T(128)S(1)}, f32[64]{0:T(128)}, u32[]{:S(2)}) copy-start(f32[64]{0:T(128)} %copy-done.11) | copy-start | bytes 772
  469.3 121.3 %all-to-all-start = ((bf16[8,1,16,10,2048]{4,2,3,1,0:T(8,128)(2,1)}), bf16[8,1,16,10,2048]{4,2,3,1,0:T(8,128)(2,1)}, u32[]{:S(2)}, u32[]{:S(2)}) async-start(bf16[8,1,16,10,2048]{4,2,3,1,0:T(8,128)(2,1)} %bitcast.113), calls=%async_computation.2 | async-start | bytes 10485760 | tf_op jit(solution)/shard_map/all_to_all | solution.py:103
  600.3 22.0 %copy-start.1 = (bf16[512,2048]{1,0:T(8,128)(2,1)S(1)}, bf16[512,2048]{1,0:T(8,128)(2,1)}, u32[]{:S(2)}) copy-start(bf16[512,2048]{1,0:T(8,128)(2,1)} %param.10) | copy-start | bytes 6291460
  610.3 11.1 %copy-start.10 = (f32[2048]{0:T(1024)S(1)}, f32[2048]{0:T(1024)}, u32[]{:S(2)}) copy-start(f32[2048]{0:T(1024)} %param.17) | copy-start | bytes 24580
  621.4 1.0 copy-start.4
Sparse Core Ops, SparseCore 0:
  11.6 27.5 reduce-scatter.2
  43.0 77.6 all-gather.1
  316.2 153.1 reduce-scatter.4

commit v2 on v1

--- a/solution.py
+++ b/solution.py
@@ -63,8 +63,12 @@
     own_onehot = own_ids[:, :, None] == expert_range[None, None, :]
     chosen = jnp.sum(jnp.where(own_onehot, logits[:, None, :], 0.0), axis=-1)
     gate_weights = jax.nn.softmax(chosen, axis=-1)
-    all_rows = lax.all_gather(normed, ("expert", "tensor"), axis=0, tiled=True)
-    all_ids = lax.all_gather(expert_ids, "expert", axis=0, tiled=True)
+    ids_wide = jnp.pad(own_ids.astype(jnp.bfloat16), ((0, 0), (0, 128 - top_count)))
+    packed = lax.all_gather(
+        jnp.concatenate([normed, ids_wide], axis=1), ("expert", "tensor"), axis=0, tiled=True
+    )
+    all_rows = packed[:, :model_width]
+    all_ids = packed[:, model_width:model_width + top_count].astype(jnp.int32)
     holds = (placement[None, :] == expert_range[:, None]).astype(jnp.int32)
     copies = jnp.sum(holds, axis=1)
     copy_rank = jnp.cumsum(holds, axis=1) - 1
@@ -72,30 +76,34 @@
     copy_pick = holder_range[:, None] % copies[None, :]
     picked = (holds[None] > 0) & (copy_rank[None] == copy_pick[:, :, None])
     slot_pick = jnp.sum(jnp.where(picked, slot_range[None, None, :], 0), axis=2)
-    flat_ids = all_ids.reshape(blocks, row_count * top_count)
+    pair_count = row_count * top_count
+    flat_ids = all_ids.reshape(blocks, pair_count)
     block_holder = jnp.arange(blocks, dtype=jnp.int32) // groups
-    block_pick = slot_pick[block_holder]
+    local_pick = jnp.where(
+        slot_pick // slot_dev == my_holder, slot_pick % slot_dev, slot_dev
+    )[block_holder]
     onehot = flat_ids[:, :, None] == expert_range
-    slot_of = jnp.sum(jnp.where(onehot, block_pick[:, None, :], 0), axis=-1)
-    slot_hot = (slot_of[:, :, None] == slot_range).astype(jnp.int32)
-    rank_all = jnp.sum(jnp.cumsum(slot_hot, axis=1) * slot_hot, axis=-1) - 1
-    holder_all = slot_of // slot_dev
-    local_all = slot_of % slot_dev
-    block_ids = jnp.arange(blocks, dtype=jnp.int32)[:, None]
-    token_of = block_ids * row_count + jnp.arange(row_count * top_count, dtype=jnp.int32)[None, :] // top_count
-    mine = holder_all == my_holder
-    row_total = blocks * slot_dev * capacity
-    target = jnp.where(mine, (block_ids * slot_dev + local_all) * capacity + rank_all, row_total)
-    index_table = jnp.zeros((row_total,), jnp.int32).at[target.reshape(-1)].set(
-        token_of.reshape(-1), mode="drop", unique_indices=True
-    )
-    received = jnp.take(all_rows, index_table, axis=0).reshape(
-        holders, groups, slot_dev, capacity, model_width
-    )
-    own_block = my_holder * groups + my_group
-    holder = lax.dynamic_index_in_dim(holder_all, own_block, 0, keepdims=False)
-    local_slot = lax.dynamic_index_in_dim(local_all, own_block, 0, keepdims=False)
-    rank_in = lax.dynamic_index_in_dim(rank_all, own_block, 0, keepdims=False)
+    local_all = jnp.sum(jnp.where(onehot, local_pick[:, None, :], 0), axis=-1)
+    local_range = jnp.arange(slot_dev, dtype=jnp.int32)
+    local_hot = (local_all[:, :, None] == local_range).astype(jnp.int32)
+    rank_all = jnp.sum(jnp.cumsum(local_hot, axis=1) * local_hot, axis=-1) - 1
+    key = jnp.where(local_all < slot_dev, local_all * capacity + rank_all, -1)
+    key = key.reshape(blocks, row_count, top_count)
+    pos_range = jnp.arange(slot_dev * capacity, dtype=jnp.int32)
+    pick_hot = jnp.any(key[:, :, :, None] == pos_range, axis=2).astype(jnp.bfloat16)
+    received = jnp.einsum(
+        "buj,bud->bjd",
+        pick_hot,
+        all_rows.reshape(blocks, row_count, model_width),
+        preferred_element_type=jnp.float32,
+    ).astype(jnp.bfloat16).reshape(holders, groups, slot_dev, capacity, model_width)
+    own_flat = own_ids.reshape(-1)
+    own_onehot_flat = own_flat[:, None] == expert_range
+    slot_of = jnp.sum(jnp.where(own_onehot_flat, slot_pick[my_holder][None, :], 0), axis=-1)
+    slot_hot = (slot_of[:, None] == slot_range).astype(jnp.int32)
+    rank_in = jnp.sum(jnp.cumsum(slot_hot, axis=0) * slot_hot, axis=-1) - 1
+    holder = slot_of // slot_dev
+    local_slot = slot_of % slot_dev
     partial_value = expert_partial(received, expert_weights)
     expert_sum = lax.psum_scatter(
         partial_value.astype(jnp.bfloat16), "tensor", scatter_dimension=1, tiled=True

time: 631 us -> 628 us (level)
  local copies, waits for them, and re-layouts: 194 us -> 101 us
  waiting for transfers between devices: 294 us -> 370 us
  blocking collectives: 30.9 us -> 0 us
  other arithmetic: 23.8 us -> 52.7 us
  matrix products: 65.5 us -> 83.4 us
    all_gather x1, waiting for transfers between devices: 0.02 us -> 77.4 us  [on_device(): lax.all_gather(jnp.concatenate([normed, ids_wide], axis=1), ('expert', 't...]
    gather x3 -> x1, local copies, waits for them, and re-layouts: 77.9 us -> 0.57 us  [on_device(): jnp.where(slot_pick // slot_dev == my_holder, slot_pick % slot_dev, slot_...]
    scatter x1 -> x0, local copies, waits for them, and re-layouts: 60.5 us -> none  [on_device(): jnp.zeros((row_total,), jnp.int32).at[target.reshape(-1)]]
    dot_general x0 -> x2, matrix products: none -> 34.9 us  [the longest x1 22.8 us: expert_partial(): jnp.einsum('nqsmd,sdf->nqsmf', block_rows, weights[:, 0], preferred_eleme...]
    reshape x0 -> x1, local copies, waits for them, and re-layouts: none -> 34 us  [on_device(): received = jnp.einsum('buj,bud->bjd', pick_hot, all_rows.reshape(blocks,...]
    another operation x3 -> x5, other arithmetic: 3.56 us -> 36.6 us
    all_gather x1 -> x0, blocking collectives: 30.9 us -> none  [on_device(): all_ids = lax.all_gather(expert_ids, 'expert', axis=0, tiled=True)]
    dot_general x1, matrix products: 39.2 us -> 21.2 us  [expert_partial(): jnp.einsum('nqsmf,sdf->nqsmd', inner_act, weights[:, 2], preferred_elemen...]
  transfers between devices with their start and end apart: 4 -> 4, of which waited for: 3 -> 4; matrix products, arithmetic and copies ran while one was open for 13% -> 1% of each run, Pallas kernels for 0% -> 0%
where the time goes in v2:
time: 628 us; the launch traced here: 627 us
  waiting for transfers between devices  370 us (59%)
  local copies, waits for them, and re-layouts  101 us (16%)
  matrix products  83.4 us (13%)
  other arithmetic  52.7 us (8%)
  between operations  14.1 us (2%)
    reduce_scatter x1, waiting for transfers between devices, on_device(): lax.psum_scatter(partial_value.astype(jnp.bfloat16), 'tensor', scatter_di...  152 us
    all_to_all x1, waiting for transfers between devices, on_device(): lax.all_to_all(expert_sum, 'expert', split_axis=0, concat_axis=0, tiled=T...  114 us
    all_gather x1, waiting for transfers between devices, on_device(): lax.all_gather(jnp.concatenate([normed, ids_wide], axis=1), ('expert', 't...  77.4 us
    another operation x5, other arithmetic  36.6 us
    reshape x1, local copies, waits for them, and re-layouts, on_device(): received = jnp.einsum('buj,bud->bjd', pick_hot, all_rows.reshape(blocks,...  34 us
    reduce_scatter x1, waiting for transfers between devices, on_device(): lax.psum_scatter(jnp.dot(context, out_proj, preferred_element_type=jnp.fl...  26.8 us
    convert_element_type x1, local copies, waits for them, and re-layouts, on_device(): partial_value.astype(jnp.bfloat16)  24.4 us
    dot_general x1, matrix products, expert_partial(): jnp.einsum('nqsmd,sdf->nqsmf', block_rows, weights[:, 0], preferred_eleme...  22.8 us
  transfers between devices with their start and end apart: 4, of which 4 were waited for; matrix products, arithmetic and copies ran while one was open for 1% of the time, Pallas kernels for 0%

profile of v2, /device:TPU:0, one launch (start us, length us, event | category | flops | bytes accessed | tf_op | source)
XLA Modules:
  0.0 626.5 jit_solution(3960092588079079939)
XLA Ops:
  7.2 1.5 copy-done
  8.8 2.7 convolution_convert_fusion.1
  11.5 0.8 constant_dynamic-slice_fusion
  12.4 26.8 %reduce-scatter.3.cloned.1.call-done = bf16[64,2048]{1,0:T(8,128)(2,1)} async-done(((bf16[256,2048]{1,0:T(8,128)(2,1)}), bf16[64,2048]{1,0:T(8,128)(2,1)}) %reduce-scatter.3.cloned.1.call-update) | async-done | bytes 262160 | tf_op jit(solution)/shard_map/reduce_scatter | solution.py:52
  39.2 1.2 multiply_reduce_fusion.1
  40.4 1.2 fusion.31
  41.6 0.7 fusion.33
  42.4 0.7 fusion.44
  43.4 0.8 fusion.43
  45.2 77.4 %all-gather.2.cloned.1.call-done = bf16[2048,2176]{1,0:T(8,128)(2,1)} async-done(((bf16[64,2176]{1,0:T(8,128)(2,1)}), bf16[2048,2176]{1,0:T(8,128)(2,1)}) %all-gather.2.cloned.1.call-update) | async-done | bytes 8912912 | tf_op jit(solution)/shard_map/all_gather | solution.py:67
  122.6 1.1 slice_convert_fusion
  124.3 1.0 select_reduce_fusion
  125.5 36.3 %reduce-window.14 = s32[32,16,4,128]{3,1,2,0:T(8,128)S(1)} reduce-window(s32[32,16,4,128]{3,1,2,0:T(8,128)S(1)} %fusion.29, s32[]{:T(128)} %constant.108.clone.1), window={size=1x1x1x128 pad=0_0x0_0x0_0x127_0}, to_apply=%region_9.10 | reduce-window | flops 33292288 | bytes 2097156 | tf_op jit(solution)/shard_map/reduce-window
  162.1 0.7 copy.68
  163.6 0.9 copy.72
  164.5 6.0 fusion.10
  170.6 8.3 %slice.43 = bf16[2048,2048]{1,0:T(8,128)(2,1)} slice(bf16[2048,2176]{1,0:T(8,128)(2,1)} %all-gather.2.cloned.1.call-done), slice={[0:2048], [0:2048]} | slice | bytes 16777216 | tf_op jit(solution)/shard_map/slice | solution.py:70
  178.9 12.1 %convolution_convert_fusion = bf16[32,160,2048]{2,1,0:T(8,128)(2,1)} fusion(pred[32,64,160]{2,1,0:T(8,128)(4,1)S(1)} %fusion.10, bf16[32,64,2048]{2,1,0:T(8,128)(2,1)} %bitcast.126), kind=kOutput, calls=%fused_computation.15 | convolution fusion | flops 1352663040 | bytes 29687808 | tf_op jit(solution)/shard_map/buj,bud->bjd/dot_general | solution.py:94
  191.0 34.0 %reshape.369 = bf16[8,4,16,10,2048]{4,3,2,1,0:T(8,128)(2,1)} reshape(bf16[32,160,2048]{2,1,0:T(8,128)(2,1)} %convolution_convert_fusion) | data formatting | bytes 41943040 | tf_op jit(solution)/shard_map/reshape | solution.py:99
  225.0 21.7 %fusion = f32[16,8,4,10,256]{4,3,2,1,0:T(8,128)} fusion(bf16[8,4,16,10,2048]{4,3,2,1,0:T(8,128)(2,1)} %reshape.369, bf16[16,3,2048,256]{3,2,1,0:T(8,128)(2,1)} %param.16), kind=kOutput, calls=%fused_computation.3 | convolution fusion | flops 5368709120 | bytes 55574528 | tf_op jit(solution)/shard_map/nqsmd,sdf->nqsmf/dot_general | solution.py:18
  246.7 22.8 %fusion.77 = bf16[8,4,16,10,256]{4,3,1,0,2:T(8,128)(2,1)} fusion(f32[16,8,4,10,256]{4,3,2,1,0:T(8,128)} %fusion, bf16[16,3,2048,256]{3,2,1,0:T(8,128)(2,1)} %param.16, bf16[8,4,16,10,2048]{4,3,2,1,0:T(8,128)(2,1)} %reshape.369), kind=kOutput, calls=%fused_computation.17.clone.clone.2 | convolution fusion | flops 5376573440 | bytes 61341696 | tf_op jit(solution)/shard_map/nqsmd,sdf->nqsmf/dot_general | solution.py:15
  269.4 21.2 %convert_bitcast_fusion = bf16[8,4,16,10,2048]{4,3,1,0,2:T(8,128)(2,1)} fusion(bf16[16,3,2048,256]{3,2,1,0:T(8,128)(2,1)} %param.16, bf16[8,4,16,10,256]{4,3,1,0,2:T(8,128)(2,1)} %fusion.77), kind=kOutput, calls=%fused_computation.2 | convolution fusion | flops 5379194880 | bytes 41943040 | tf_op jit(solution)/shard_map/nqsmf,sdf->nqsmd/dot_general | solution.py:22
  290.7 24.4 %copy.79 = bf16[8,4,16,10,2048]{4,2,3,0,1:T(8,128)(2,1)} copy(bf16[8,4,16,10,2048]{4,3,1,0,2:T(8,128)(2,1)} %convert_bitcast_fusion) | data formatting | bytes 41943040 | tf_op jit(solution)/shard_map/convert_element_type | solution.py:109
  315.1 151.8 %reduce-scatter.5.cloned.1.call-done = bf16[8,1,16,10,2048]{4,2,3,0,1:T(8,128)(2,1)} async-done(((bf16[8,4,16,10,2048]{4,2,3,0,1:T(8,128)(2,1)}), bf16[8,1,16,10,2048]{4,2,3,0,1:T(8,128)(2,1)}) %reduce-scatter.5.cloned.1.call-update) | async-done | bytes 5242896 | tf_op jit(solution)/shard_map/reduce_scatter | solution.py:108
  466.9 5.5 all-to-all-start
  473.4 0.7 fusion.32
  474.7 113.6 %all-to-all-done = bf16[8,1,16,10,2048]{4,2,3,1,0:T(8,128)(2,1)} async-done(((bf16[8,1,16,10,2048]{4,2,3,1,0:T(8,128)(2,1)}), bf16[8,1,16,10,2048]{4,2,3,1,0:T(8,128)(2,1)}, u32[]{:S(2)}, u32[]{:S(2)}) %all-to-all-start) | async-done | bytes 5242912 | tf_op jit(solution)/shard_map/all_to_all | solution.py:111
  588.2 9.7 %copy.81 = bf16[8,1,16,10,2048]{4,3,2,0,1:T(8,128)(2,1)} copy(bf16[8,1,16,10,2048]{4,2,3,1,0:T(8,128)(2,1)} %all-to-all-done) | data formatting | bytes 10485760 | tf_op jit(solution)/shard_map/all_to_all | solution.py:111
  598.0 10.0 %reshape.344 = bf16[1280,2048]{1,0:T(8,128)(2,1)} reshape(bf16[8,1,16,10,2048]{4,3,2,0,1:T(8,128)(2,1)} %copy.81) | data formatting | bytes 10485760 | tf_op jit(solution)/shard_map/reshape | solution.py:113
  608.0 8.5 %gather_fusion.1 = bf16[512,2048]{1,0:T(8,128)(2,1)} fusion(bf16[1280,2048]{1,0:T(8,128)(2,1)} %reshape.344, s32[1024]{0:T(1024)S(1)} %pad_clamp_fusion), kind=kCustom, calls=%fused_computation.1 | custom fusion | bytes 4196352 | tf_op jit(solution)/shard_map/gather | solution.py:113
  616.4 2.3 fusion.25
  619.0 0.9 multiply_multiply_fusion
  (67 shorter events, 5.2 us)
Async XLA Ops:
  7.2 1.6 copy-start
  7.2 32.0 %reduce-scatter.3.cloned.1.call-start = ((), (), s32[]{:S(2)}) async-start(), calls=%async_computation.3 | async-start | bytes 1310720 | tf_op jit(solution)/shard_map/reduce_scatter | solution.py:52
  11.4 111.2 %all-gather.2.cloned.1.call-start = ((), (), s32[]{:S(2)}) async-start(), calls=%async_computation.4 | async-start | bytes 9191424 | tf_op jit(solution)/shard_map/all_gather | solution.py:67
  42.3 424.6 %reduce-scatter.5.cloned.1.call-start = ((), (), s32[]{:S(2)}) async-start(), calls=%async_computation.5 | async-start | bytes 26214400 | tf_op jit(solution)/shard_map/reduce_scatter | solution.py:108
  315.1 158.3 %copy-start.2 = (bf16[64,2048]{1,0:T(8,128)(2,1)S(1)}, bf16[64,2048]{1,0:T(8,128)(2,1)}, u32[]{:S(2)}) copy-start(bf16[64,2048]{1,0:T(8,128)(2,1)} %param.11) | copy-start | bytes 786436
  315.1 158.3 %copy-start.3 = (bf16[64,2048]{1,0:T(8,128)(2,1)S(1)}, bf16[64,2048]{1,0:T(8,128)(2,1)}, u32[]{:S(2)}) copy-start(bf16[64,2048]{1,0:T(8,128)(2,1)} %reduce-scatter.3.cloned.1.call-done) | copy-start | bytes 786436
  315.1 158.3 %copy-start.5 = (f32[2048,64]{0,1:T(8,128)S(1)}, f32[2048,64]{0,1:T(8,128)}, u32[]{:S(2)}) copy-start(f32[2048,64]{0,1:T(8,128)} %param.13) | copy-start | bytes 1572868
  315.1 158.3 %copy-start.6 = (f32[2048]{0:T(1024)S(1)}, f32[2048]{0:T(1024)}, u32[]{:S(2)}) copy-start(f32[2048]{0:T(1024)} %param.12) | copy-start | bytes 24580
  466.9 121.3 %all-to-all-start = ((bf16[8,1,16,10,2048]{4,2,3,1,0:T(8,128)(2,1)}), bf16[8,1,16,10,2048]{4,2,3,1,0:T(8,128)(2,1)}, u32[]{:S(2)}, u32[]{:S(2)}) async-start(bf16[8,1,16,10,2048]{4,2,3,1,0:T(8,128)(2,1)} %bitcast.127), calls=%async_computation.2 | async-start | bytes 10485760 | tf_op jit(solution)/shard_map/all_to_all | solution.py:111
  598.0 22.0 %copy-start.1 = (bf16[512,2048]{1,0:T(8,128)(2,1)S(1)}, bf16[512,2048]{1,0:T(8,128)(2,1)}, u32[]{:S(2)}) copy-start(bf16[512,2048]{1,0:T(8,128)(2,1)} %param.10) | copy-start | bytes 6291460
  608.0 11.1 %copy-start.7 = (f32[2048]{0:T(1024)S(1)}, f32[2048]{0:T(1024)}, u32[]{:S(2)}) copy-start(f32[2048]{0:T(1024)} %param.17) | copy-start | bytes 24580
  619.0 1.0 copy-start.4
Sparse Core Ops, SparseCore 0:
  11.6 27.5 reduce-scatter.2
  43.0 79.5 all-gather.1
  315.2 151.7 reduce-scatter.4

commit v3 on v1

--- a/solution.py
+++ b/solution.py
@@ -63,8 +63,17 @@
     own_onehot = own_ids[:, :, None] == expert_range[None, None, :]
     chosen = jnp.sum(jnp.where(own_onehot, logits[:, None, :], 0.0), axis=-1)
     gate_weights = jax.nn.softmax(chosen, axis=-1)
-    all_rows = lax.all_gather(normed, ("expert", "tensor"), axis=0, tiled=True)
-    all_ids = lax.all_gather(expert_ids, "expert", axis=0, tiled=True)
+    gate_hi = gate_weights.astype(jnp.bfloat16)
+    gate_lo = (gate_weights - gate_hi.astype(jnp.float32)).astype(jnp.bfloat16)
+    side = jnp.concatenate([own_ids.astype(jnp.bfloat16), gate_hi, gate_lo], axis=1)
+    side = jnp.pad(side, ((0, 0), (0, 128 - 3 * top_count)))
+    packed = lax.all_gather(
+        jnp.concatenate([normed, side], axis=1), ("expert", "tensor"), axis=0, tiled=True
+    ).reshape(blocks, row_count, model_width + 128)
+    all_rows = packed[:, :, :model_width]
+    all_ids = packed[:, :, model_width:model_width + top_count].astype(jnp.int32)
+    all_hi = packed[:, :, model_width + top_count:model_width + 2 * top_count]
+    all_lo = packed[:, :, model_width + 2 * top_count:model_width + 3 * top_count]
     holds = (placement[None, :] == expert_range[:, None]).astype(jnp.int32)
     copies = jnp.sum(holds, axis=1)
     copy_rank = jnp.cumsum(holds, axis=1) - 1
@@ -72,40 +81,58 @@
     copy_pick = holder_range[:, None] % copies[None, :]
     picked = (holds[None] > 0) & (copy_rank[None] == copy_pick[:, :, None])
     slot_pick = jnp.sum(jnp.where(picked, slot_range[None, None, :], 0), axis=2)
-    flat_ids = all_ids.reshape(blocks, row_count * top_count)
+    local_range = jnp.arange(slot_dev, dtype=jnp.int32)
+    mine_map = (slot_pick[:, :, None] == my_holder * slot_dev + local_range).astype(jnp.bfloat16)
     block_holder = jnp.arange(blocks, dtype=jnp.int32) // groups
-    block_pick = slot_pick[block_holder]
-    onehot = flat_ids[:, :, None] == expert_range
-    slot_of = jnp.sum(jnp.where(onehot, block_pick[:, None, :], 0), axis=-1)
-    slot_hot = (slot_of[:, :, None] == slot_range).astype(jnp.int32)
-    rank_all = jnp.sum(jnp.cumsum(slot_hot, axis=1) * slot_hot, axis=-1) - 1
-    holder_all = slot_of // slot_dev
-    local_all = slot_of % slot_dev
-    block_ids = jnp.arange(blocks, dtype=jnp.int32)[:, None]
-    token_of = block_ids * row_count + jnp.arange(row_count * top_count, dtype=jnp.int32)[None, :] // top_count
-    mine = holder_all == my_holder
-    row_total = blocks * slot_dev * capacity
-    target = jnp.where(mine, (block_ids * slot_dev + local_all) * capacity + rank_all, row_total)
-    index_table = jnp.zeros((row_total,), jnp.int32).at[target.reshape(-1)].set(
-        token_of.reshape(-1), mode="drop", unique_indices=True
+    block_map = mine_map[block_holder]
+    names = all_ids[:, :, :, None] == expert_range
+    name_hot = jnp.any(names, axis=2).astype(jnp.bfloat16)
+    gate_e_hi = jnp.sum(jnp.where(names, all_hi[:, :, :, None], 0), axis=2).astype(jnp.bfloat16)
+    gate_e_lo = jnp.sum(jnp.where(names, all_lo[:, :, :, None], 0), axis=2).astype(jnp.bfloat16)
+    stack = jnp.concatenate([name_hot, gate_e_hi, gate_e_lo], axis=1)
+    per_slot = jnp.einsum("bue,bes->bus", stack, block_map, preferred_element_type=jnp.float32)
+    token_hit = per_slot[:, :row_count]
+    gate_sel_hi = per_slot[:, row_count:2 * row_count]
+    gate_sel_lo = per_slot[:, 2 * row_count:]
+    token_range = jnp.arange(row_count, dtype=jnp.int32)
+    earlier = (token_range[None, :] < token_range[:, None]).astype(jnp.bfloat16)
+    count_before = jnp.einsum(
+        "uv,bvs->bus", earlier, token_hit.astype(jnp.bfloat16), preferred_element_type=jnp.float32
     )
-    received = jnp.take(all_rows, index_table, axis=0).reshape(
-        holders, groups, slot_dev, capacity, model_width
-    )
-    own_block = my_holder * groups + my_group
-    holder = lax.dynamic_index_in_dim(holder_all, own_block, 0, keepdims=False)
-    local_slot = lax.dynamic_index_in_dim(local_all, own_block, 0, keepdims=False)
-    rank_in = lax.dynamic_index_in_dim(rank_all, own_block, 0, keepdims=False)
-    partial_value = expert_partial(received, expert_weights)
-    expert_sum = lax.psum_scatter(
-        partial_value.astype(jnp.bfloat16), "tensor", scatter_dimension=1, tiled=True
-    )
-    returned = lax.all_to_all(expert_sum, "expert", split_axis=0, concat_axis=0, tiled=True)
-    own_index = (holder * slot_dev + local_slot) * capacity + rank_in
-    outputs = returned.reshape(-1, model_width)[own_index].reshape(
-        row_count, top_count, model_width
-    )
-    moe_sum = jnp.einsum("rk,rkd->rd", gate_weights, outputs.astype(jnp.float32))
+    rank_range = jnp.arange(capacity, dtype=jnp.float32)
+    pick = token_hit[..., None] * (count_before[..., None] == rank_range)
+    pick_hot = pick.astype(jnp.bfloat16)
+    received = jnp.einsum(
+        "busr,bud->bsrd", pick_hot, all_rows, preferred_element_type=jnp.float32
+    ).astype(jnp.bfloat16).reshape(holders, groups, slot_dev, capacity, model_width)
+    partial_value = expert_partial(received, expert_weights).astype(jnp.bfloat16)
+    if blocks * row_count * model_width * 4 <= (32 << 20):
+        partial_value = partial_value.reshape(blocks, slot_dev, capacity, model_width)
+        weight_hi = (pick * gate_sel_hi[..., None]).astype(jnp.bfloat16)
+        weight_lo = (pick * gate_sel_lo[..., None]).astype(jnp.bfloat16)
+        weight_both = jnp.concatenate([weight_hi, weight_lo], axis=1)
+        combined = jnp.einsum(
+            "busr,bsrd->bud", weight_both, partial_value, preferred_element_type=jnp.float32
+        )
+        token_sum = (combined[:, :row_count] + combined[:, row_count:]).reshape(-1, model_width)
+        moe_sum = lax.psum_scatter(
+            token_sum, ("expert", "tensor"), scatter_dimension=0, tiled=True
+        )
+    else:
+        expert_sum = lax.psum_scatter(partial_value, "tensor", scatter_dimension=1, tiled=True)
+        returned = lax.all_to_all(expert_sum, "expert", split_axis=0, concat_axis=0, tiled=True)
+        own_flat = own_ids.reshape(-1)
+        own_onehot_flat = own_flat[:, None] == expert_range
+        slot_of = jnp.sum(
+            jnp.where(own_onehot_flat, slot_pick[my_holder][None, :], 0), axis=-1
+        )
+        slot_hot = (slot_of[:, None] == slot_range).astype(jnp.int32)
+        rank_in = jnp.sum(jnp.cumsum(slot_hot, axis=0) * slot_hot, axis=-1) - 1
+        own_index = slot_of * capacity + rank_in
+        outputs = returned.reshape(-1, model_width)[own_index].reshape(
+            row_count, top_count, model_width
+        )
+        moe_sum = jnp.einsum("rk,rkd->rd", gate_weights, outputs.astype(jnp.float32))
     hidden_out = hidden_mid + moe_sum
     normed_out = rms_scale(hidden_out, post_gain)
     return (hidden_out, normed_out)

time: 631 us -> 471 us (0.75)
  local copies, waits for them, and re-layouts: 194 us -> 3.72 us
  matrix products: 65.5 us -> 126 us
  blocking collectives: 30.9 us -> 0 us
  other arithmetic: 23.8 us -> 40.9 us
  waiting for transfers between devices: 294 us -> 285 us
    all_to_all x1 -> x0, waiting for transfers between devices: 113 us -> none  [on_device(): lax.all_to_all(expert_sum, 'expert', split_axis=0, concat_axis=0, tiled=T...]
    gather x4 -> x1, local copies, waits for them, and re-layouts: 86.4 us -> 0.59 us  [on_device(): block_map = mine_map[block_holder]]
    all_gather x1, waiting for transfers between devices: 0.02 us -> 76.7 us  [on_device(): lax.all_gather(jnp.concatenate([normed, side], axis=1), ('expert', 'tenso...]
    dot_general x1 -> x5, matrix products: 2.28 us -> 72.9 us  [the longest x1 31 us: on_device(): jnp.einsum('busr,bsrd->bud', weight_both, partial_value, preferred_elemen...]
    scatter x1 -> x0, local copies, waits for them, and re-layouts: 60.5 us -> none  [on_device(): jnp.zeros((row_total,), jnp.int32).at[target.reshape(-1)]]
    all_gather x1 -> x0, blocking collectives: 30.9 us -> none  [on_device(): all_ids = lax.all_gather(expert_ids, 'expert', axis=0, tiled=True)]
    reduce_scatter x1, waiting for transfers between devices: 153 us -> 182 us  [on_device(): lax.psum_scatter(token_sum, ('expert', 'tensor'), scatter_dimension=0, ti...]
    convert_element_type x1 -> x0, local copies, waits for them, and re-layouts: 24.3 us -> none  [on_device(): partial_value.astype(jnp.bfloat16)]
  transfers between devices with their start and end apart: 4 -> 3, of which waited for: 3 -> 3; matrix products, arithmetic and copies ran while one was open for 13% -> 1% of each run, Pallas kernels for 0% -> 0%
where the time goes in v3:
time: 471 us; the launch traced here: 470 us
  waiting for transfers between devices  285 us (61%)
  matrix products  126 us (27%)
  other arithmetic  40.9 us (9%)
  between operations  14 us (3%)
    reduce_scatter x1, waiting for transfers between devices, on_device(): lax.psum_scatter(token_sum, ('expert', 'tensor'), scatter_dimension=0, ti...  182 us
    all_gather x1, waiting for transfers between devices, on_device(): lax.all_gather(jnp.concatenate([normed, side], axis=1), ('expert', 'tenso...  76.7 us
    dot_general x1, matrix products, on_device(): jnp.einsum('busr,bsrd->bud', weight_both, partial_value, preferred_elemen...  31 us
    dot_general x1, matrix products, expert_partial(): jnp.einsum('nqsmd,sdf->nqsmf', block_rows, weights[:, 0], preferred_eleme...  27.7 us
    dot_general x1, matrix products, expert_partial(): jnp.einsum('nqsmd,sdf->nqsmf', block_rows, weights[:, 1], preferred_eleme...  27 us
    reduce_scatter x1, waiting for transfers between devices, on_device(): lax.psum_scatter(jnp.dot(context, out_proj, preferred_element_type=jnp.fl...  26.8 us
    dot_general x1, matrix products, expert_partial(): jnp.einsum('nqsmf,sdf->nqsmd', inner_act, weights[:, 2], preferred_elemen...  21.2 us
    add x1, other arithmetic, on_device(): combined[:, :row_count] + combined[:, row_count:]  17.5 us
  transfers between devices with their start and end apart: 3, of which 3 were waited for; matrix products, arithmetic and copies ran while one was open for 1% of the time, Pallas kernels for 0%

profile of v3, /device:TPU:0, one launch (start us, length us, event | category | flops | bytes accessed | tf_op | source)
XLA Modules:
  0.0 469.7 jit_solution(5206277196794099286)
XLA Ops:
  7.2 1.5 copy-done
  8.8 2.7 convolution_convert_fusion.2
  11.5 0.8 fusion.73
  12.3 26.8 %reduce-scatter.3.cloned.1.call-done = bf16[64,2048]{1,0:T(8,128)(2,1)} async-done(((bf16[256,2048]{1,0:T(8,128)(2,1)}), bf16[64,2048]{1,0:T(8,128)(2,1)}) %reduce-scatter.3.cloned.1.call-update) | async-done | bytes 262160 | tf_op jit(solution)/shard_map/reduce_scatter | solution.py:52
  39.2 1.2 multiply_reduce_fusion.1
  40.4 1.9 fusion.49
  42.3 0.2 select_reduce_fusion.1
  42.9 1.2 fusion.50
  44.0 0.7 fusion.51
  44.8 0.7 fusion.59
  45.5 0.3 reduce_window_sum.11
  45.8 0.8 fusion.58
  46.8 0.3 select_reduce_fusion
  47.2 0.6 gather_fusion
  47.8 76.7 %all-gather.2.cloned.1.call-done = bf16[2048,2176]{1,0:T(8,128)(2,1)} async-done(((bf16[64,2176]{1,0:T(8,128)(2,1)}), bf16[2048,2176]{1,0:T(8,128)(2,1)}) %all-gather.2.cloned.1.call-update) | async-done | bytes 8912912 | tf_op jit(solution)/shard_map/all_gather | solution.py:70
  124.5 2.1 fusion.74
  126.6 3.7 fusion.21
  130.3 0.4 copy.65
  130.8 8.1 %fusion.30 = (bf16[32,64,64]{2,1,0:T(8,128)(2,1)S(1)}, bf16[32,64,64]{2,1,0:T(8,128)(2,1)S(1)}) fusion(s32[32,64,8]{2,1,0:T(8,128)S(1)} %get-tuple-element.10, bf16[32,64,8]{2,1,0:T(8,128)(2,1)S(1)} %get-tuple-element.9, bf16[32,64,8]{2,1,0:T(8,128)(2,1)S(1)} %get-tuple-element.8), kind=kLoop, calls=%fused_computation.32 | loop fusion | flops 4980736 | bytes 655360 | tf_op jit(solution)/shard_map/reduce_sum | solution.py:90
  138.9 0.3 copy.66
  139.3 0.3 copy.67
  139.6 0.6 fusion.41
  140.7 13.4 %convolution_convert_fusion.1 = bf16[32,16,10,2048]{3,1,2,0:T(8,128)(2,1)} fusion(bf16[32,64,2176]{2,1,0:T(8,128)(2,1)} %bitcast.98, f32[32,64,16]{1,2,0:T(8,128)S(1)} %get-tuple-element.15, f32[32,64,16]{1,2,0:T(8,128)S(1)} %copy.69), kind=kOutput, calls=%fused_computation.16 | convolution fusion | flops 1353318400 | bytes 29622272 | tf_op jit(solution)/shard_map/busr,bud->bsrd/dot_general | solution.py:105
  154.1 27.0 %fusion = f32[16,8,4,10,256]{4,3,2,1,0:T(8,128)} fusion(bf16[8,4,16,10,2048]{4,2,3,1,0:T(8,128)(2,1)} %bitcast.95, bf16[16,3,2048,256]{3,2,1,0:T(8,128)(2,1)} %param.16), kind=kOutput, calls=%fused_computation.1 | convolution fusion | flops 5368709120 | bytes 42991616 | tf_op jit(solution)/shard_map/nqsmd,sdf->nqsmf/dot_general | solution.py:18
  181.1 27.7 %fusion.15.clone.5 = bf16[8,4,16,10,256]{4,3,1,0,2:T(8,128)(2,1)} fusion(f32[16,8,4,10,256]{4,3,2,1,0:T(8,128)} %fusion, bf16[16,3,2048,256]{3,2,1,0:T(8,128)(2,1)} %param.16, bf16[8,4,16,10,2048]{4,2,3,1,0:T(8,128)(2,1)} %bitcast.96), kind=kOutput, calls=%fused_computation.19.clone.clone.clone.2 | convolution fusion | flops 5376573440 | bytes 48758784 | tf_op jit(solution)/shard_map/nqsmd,sdf->nqsmf/dot_general | solution.py:15
  208.8 21.2 %convolution_convert_fusion = bf16[16,8,4,10,2048]{4,3,2,1,0:T(8,128)(2,1)} fusion(bf16[16,3,2048,256]{3,2,1,0:T(8,128)(2,1)} %param.16, bf16[8,4,16,10,256]{4,3,1,0,2:T(8,128)(2,1)} %fusion.15.clone.5), kind=kOutput, calls=%fused_computation.7 | convolution fusion | flops 5379194880 | bytes 41943040 | tf_op jit(solution)/shard_map/nqsmf,sdf->nqsmd/dot_general | solution.py:22
  230.0 0.6 fusion.33
  230.7 31.0 %fusion.6 = f32[32,128,2048]{2,1,0:T(8,128)} fusion(bf16[32,16,10,2048]{3,2,0,1:T(8,128)(2,1)} %bitcast.93, bf16[32,64,16,10]{1,2,3,0:T(8,128)(2,1)S(1)} %get-tuple-element.12, bf16[32,64,16,10]{1,2,3,0:T(8,128)(2,1)S(1)} %get-tuple-element.11), kind=kOutput, calls=%fused_computation.8 | convolution fusion | flops 2686976000 | bytes 55836672 | tf_op jit(solution)/shard_map/busr,bsrd->bud/dot_general | solution.py:114
  261.7 17.5 %slice_add_fusion = f32[32,64,2048]{2,1,0:T(8,128)} fusion(f32[32,128,2048]{2,1,0:T(8,128)} %fusion.6), kind=kLoop, calls=%fused_computation.9 | loop fusion | flops 4194304 | bytes 50331648 | tf_op jit(solution)/shard_map/add | solution.py:117
  279.2 181.8 %reduce-scatter.5.cloned.1.call-done = f32[64,2048]{1,0:T(8,128)} async-done(((f32[2048,2048]{1,0:T(8,128)}), f32[64,2048]{1,0:T(8,128)}) %reduce-scatter.5.cloned.1.call-update) | async-done | bytes 524304 | tf_op jit(solution)/shard_map/reduce_scatter | solution.py:118
  461.0 1.2 multiply_reduce_fusion
  462.2 0.9 multiply_multiply_fusion
  (39 shorter events, 1.5 us)
Async XLA Ops:
  7.2 1.6 copy-start
  7.2 32.0 %reduce-scatter.3.cloned.1.call-start = ((), (), s32[]{:S(2)}) async-start(), calls=%async_computation.2 | async-start | bytes 1310720 | tf_op jit(solution)/shard_map/reduce_scatter | solution.py:52
  11.4 113.0 %all-gather.2.cloned.1.call-start = ((), (), s32[]{:S(2)}) async-start(), calls=%async_computation.3 | async-start | bytes 9191424 | tf_op jit(solution)/shard_map/all_gather | solution.py:70
  44.8 416.2 %reduce-scatter.5.cloned.1.call-start = ((), (), s32[]{:S(2)}) async-start(), calls=%async_computation.4 | async-start | bytes 17301504 | tf_op jit(solution)/shard_map/reduce_scatter | solution.py:118
  279.1 184.1 %copy-start.1 = (bf16[512,2048]{1,0:T(8,128)(2,1)S(1)}, bf16[512,2048]{1,0:T(8,128)(2,1)}, u32[]{:S(2)}) copy-start(bf16[512,2048]{1,0:T(8,128)(2,1)} %param.10) | copy-start | bytes 6291460
  279.1 181.8 %copy-start.2 = (bf16[64,2048]{1,0:T(8,128)(2,1)S(1)}, bf16[64,2048]{1,0:T(8,128)(2,1)}, u32[]{:S(2)}) copy-start(bf16[64,2048]{1,0:T(8,128)(2,1)} %param.11) | copy-start | bytes 786436
  279.1 181.8 %copy-start.3 = (bf16[64,2048]{1,0:T(8,128)(2,1)S(1)}, bf16[64,2048]{1,0:T(8,128)(2,1)}, u32[]{:S(2)}) copy-start(bf16[64,2048]{1,0:T(8,128)(2,1)} %reduce-scatter.3.cloned.1.call-done) | copy-start | bytes 786436
  279.1 183.1 %copy-start.5 = (f32[2048]{0:T(1024)S(1)}, f32[2048]{0:T(1024)}, u32[]{:S(2)}) copy-start(f32[2048]{0:T(1024)} %param.17) | copy-start | bytes 24580
  462.2 1.0 copy-start.4
Sparse Core Ops, SparseCore 0:
  11.6 27.5 reduce-scatter.2
  44.9 79.5 all-gather.1
  279.3 181.6 reduce-scatter.4

commit v4 on v3

--- a/solution.py
+++ b/solution.py
@@ -110,14 +110,15 @@
         partial_value = partial_value.reshape(blocks, slot_dev, capacity, model_width)
         weight_hi = (pick * gate_sel_hi[..., None]).astype(jnp.bfloat16)
         weight_lo = (pick * gate_sel_lo[..., None]).astype(jnp.bfloat16)
-        weight_both = jnp.concatenate([weight_hi, weight_lo], axis=1)
         combined = jnp.einsum(
-            "busr,bsrd->bud", weight_both, partial_value, preferred_element_type=jnp.float32
+            "busr,bsrd->bud", weight_hi, partial_value, preferred_element_type=jnp.float32
+        ) + jnp.einsum(
+            "busr,bsrd->bud", weight_lo, partial_value, preferred_element_type=jnp.float32
         )
-        token_sum = (combined[:, :row_count] + combined[:, row_count:]).reshape(-1, model_width)
+        token_sum = combined.astype(jnp.bfloat16).reshape(-1, model_width)
         moe_sum = lax.psum_scatter(
             token_sum, ("expert", "tensor"), scatter_dimension=0, tiled=True
-        )
+        ).astype(jnp.float32)
     else:
         expert_sum = lax.psum_scatter(partial_value, "tensor", scatter_dimension=1, tiled=True)
         returned = lax.all_to_all(expert_sum, "expert", split_axis=0, concat_axis=0, tiled=True)

time: 471 us -> 439 us (0.932)
  waiting for transfers between devices: 285 us -> 251 us
  matrix products: 126 us -> 147 us
  other arithmetic: 40.9 us -> 22.7 us
    reduce_scatter x1, waiting for transfers between devices: 182 us -> 148 us  [on_device(): lax.psum_scatter(token_sum, ('expert', 'tensor'), scatter_dimension=0, ti...]
    dot_general x1 -> x2, matrix products: 31 us -> 52 us  [the longest x1 26.6 us: on_device(): jnp.einsum('busr,bsrd->bud', weight_hi, partial_value, preferred_element_...]
    add x1 -> x0, other arithmetic: 17.5 us -> none  [on_device(): combined[:, :row_count] + combined[:, row_count:]]
where the time goes in v4:
time: 439 us; the launch traced here: 438 us
  waiting for transfers between devices  251 us (57%)
  matrix products  147 us (33%)
  other arithmetic  22.7 us (5%)
  between operations  14 us (3%)
    reduce_scatter x1, waiting for transfers between devices, on_device(): lax.psum_scatter(token_sum, ('expert', 'tensor'), scatter_dimension=0, ti...  148 us
    all_gather x1, waiting for transfers between devices, on_device(): lax.all_gather(jnp.concatenate([normed, side], axis=1), ('expert', 'tenso...  76.7 us
    dot_general x1, matrix products, expert_partial(): jnp.einsum('nqsmd,sdf->nqsmf', block_rows, weights[:, 0], preferred_eleme...  27.7 us
    dot_general x1, matrix products, expert_partial(): jnp.einsum('nqsmd,sdf->nqsmf', block_rows, weights[:, 1], preferred_eleme...  27 us
    reduce_scatter x1, waiting for transfers between devices, on_device(): lax.psum_scatter(jnp.dot(context, out_proj, preferred_element_type=jnp.fl...  26.8 us
    dot_general x1, matrix products, on_device(): jnp.einsum('busr,bsrd->bud', weight_hi, partial_value, preferred_element_...  26.6 us
    dot_general x1, matrix products, on_device(): jnp.einsum('busr,bsrd->bud', weight_lo, partial_value, preferred_element_...  25.3 us
    dot_general x1, matrix products, expert_partial(): jnp.einsum('nqsmf,sdf->nqsmd', inner_act, weights[:, 2], preferred_elemen...  21.2 us
  transfers between devices with their start and end apart: 3, of which 3 were waited for; matrix products, arithmetic and copies ran while one was open for 1% of the time, Pallas kernels for 0%

profile of v4, /device:TPU:0, one launch (start us, length us, event | category | flops | bytes accessed | tf_op | source)
XLA Modules:
  0.0 438.4 jit_solution(18113725623026881318)
XLA Ops:
  7.2 1.5 copy-done
  8.8 2.7 convolution_convert_fusion.2
  11.5 0.8 fusion.81
  12.3 26.8 %reduce-scatter.3.cloned.1.call-done = bf16[64,2048]{1,0:T(8,128)(2,1)} async-done(((bf16[256,2048]{1,0:T(8,128)(2,1)}), bf16[64,2048]{1,0:T(8,128)(2,1)}) %reduce-scatter.3.cloned.1.call-update) | async-done | bytes 262160 | tf_op jit(solution)/shard_map/reduce_scatter | solution.py:52
  39.2 1.2 multiply_reduce_fusion.1
  40.4 1.9 fusion.57
  42.3 0.2 select_reduce_fusion.1
  42.9 1.2 fusion.58
  44.0 0.7 fusion.59
  44.8 0.7 fusion.67
  45.5 0.3 reduce_window_sum.11
  45.8 0.8 fusion.66
  46.8 0.3 select_reduce_fusion
  47.2 0.6 gather_fusion
  47.8 76.7 %all-gather.2.cloned.1.call-done = bf16[2048,2176]{1,0:T(8,128)(2,1)} async-done(((bf16[64,2176]{1,0:T(8,128)(2,1)}), bf16[2048,2176]{1,0:T(8,128)(2,1)}) %all-gather.2.cloned.1.call-update) | async-done | bytes 8912912 | tf_op jit(solution)/shard_map/all_gather | solution.py:70
  124.5 2.1 fusion.82
  126.6 3.7 fusion.21
  130.3 0.4 copy.70
  130.8 8.1 %fusion.30 = (bf16[32,64,64]{2,1,0:T(8,128)(2,1)S(1)}, bf16[32,64,64]{2,1,0:T(8,128)(2,1)S(1)}) fusion(s32[32,64,8]{2,1,0:T(8,128)S(1)} %get-tuple-element.10, bf16[32,64,8]{2,1,0:T(8,128)(2,1)S(1)} %get-tuple-element.9, bf16[32,64,8]{2,1,0:T(8,128)(2,1)S(1)} %get-tuple-element.8), kind=kLoop, calls=%fused_computation.34 | loop fusion | flops 4980736 | bytes 655360 | tf_op jit(solution)/shard_map/reduce_sum | solution.py:90
  138.9 0.3 copy.71
  139.3 0.3 copy.72
  139.6 0.6 fusion.50
  140.4 0.2 convolution_bitcast_fusion
  140.7 13.4 %convolution_convert_fusion.1 = bf16[32,16,10,2048]{3,1,2,0:T(8,128)(2,1)} fusion(bf16[32,64,2176]{2,1,0:T(8,128)(2,1)} %bitcast.104, f32[32,64,16]{1,2,0:T(8,128)S(1)} %get-tuple-element.13, f32[32,64,16]{1,2,0:T(8,128)S(1)} %copy.74), kind=kOutput, calls=%fused_computation.14 | convolution fusion | flops 1353318400 | bytes 29622272 | tf_op jit(solution)/shard_map/busr,bud->bsrd/dot_general | solution.py:105
  154.1 27.0 %fusion = f32[16,8,4,10,256]{4,3,2,1,0:T(8,128)} fusion(bf16[8,4,16,10,2048]{4,2,3,1,0:T(8,128)(2,1)} %bitcast.101, bf16[16,3,2048,256]{3,2,1,0:T(8,128)(2,1)} %param.16), kind=kOutput, calls=%fused_computation.1 | convolution fusion | flops 5368709120 | bytes 42991616 | tf_op jit(solution)/shard_map/nqsmd,sdf->nqsmf/dot_general | solution.py:18
  181.1 27.7 %fusion.15.clone.5 = bf16[8,4,16,10,256]{4,3,1,0,2:T(8,128)(2,1)} fusion(f32[16,8,4,10,256]{4,3,2,1,0:T(8,128)} %fusion, bf16[16,3,2048,256]{3,2,1,0:T(8,128)(2,1)} %param.16, bf16[8,4,16,10,2048]{4,2,3,1,0:T(8,128)(2,1)} %bitcast.102), kind=kOutput, calls=%fused_computation.21.clone.clone.clone.2 | convolution fusion | flops 5376573440 | bytes 48758784 | tf_op jit(solution)/shard_map/nqsmd,sdf->nqsmf/dot_general | solution.py:15
  208.8 21.2 %convolution_convert_fusion = bf16[16,8,4,10,2048]{4,3,2,1,0:T(8,128)(2,1)} fusion(bf16[16,3,2048,256]{3,2,1,0:T(8,128)(2,1)} %param.16, bf16[8,4,16,10,256]{4,3,1,0,2:T(8,128)(2,1)} %fusion.15.clone.5), kind=kOutput, calls=%fused_computation.5 | convolution fusion | flops 5379194880 | bytes 41943040 | tf_op jit(solution)/shard_map/nqsmf,sdf->nqsmd/dot_general | solution.py:22
  230.0 25.3 %fusion.11 = f32[32,64,2048,1]{2,1,3,0:T(8,128)} fusion(bf16[32,16,10,2048]{3,2,0,1:T(8,128)(2,1)} %bitcast.98, f32[32,64,16]{1,2,0:T(8,128)S(1)} %get-tuple-element.12, f32[32,64,16]{1,2,0:T(8,128)S(1)} %get-tuple-element.13, f32[32,64,16]{1,2,0:T(8,128)S(1)} %copy.74), kind=kOutput, calls=%fused_computation.15 | convolution fusion | flops 1343488000 | bytes 38141952 | tf_op jit(solution)/shard_map/busr,bsrd->bud/dot_general | solution.py:115
  255.3 26.6 %fusion.7 = bf16[32,64,2048]{2,1,0:T(8,128)(2,1)} fusion(f32[32,64,2048,1]{2,1,3,0:T(8,128)} %fusion.11, bf16[32,16,10,2048]{3,2,0,1:T(8,128)(2,1)} %bitcast.99, f32[32,64,16]{1,2,0:T(8,128)S(1)} %get-tuple-element.11, f32[32,64,16]{1,2,0:T(8,128)S(1)} %get-tuple-element.13, f32[32,64,16]{1,2,0:T(8,128)S(1)} %copy.74), kind=kOutput, calls=%fused_computation.10 | convolution fusion | flops 1351876608 | bytes 46530560 | tf_op jit(solution)/shard_map/busr,bsrd->bud/dot_general | solution.py:113
  282.0 147.7 %reduce-scatter.5.cloned.1.call-done = bf16[64,2048]{1,0:T(8,128)(2,1)} async-done(((bf16[2048,2048]{1,0:T(8,128)(2,1)}), bf16[64,2048]{1,0:T(8,128)(2,1)}) %reduce-scatter.5.cloned.1.call-update) | async-done | bytes 262160 | tf_op jit(solution)/shard_map/reduce_scatter | solution.py:119
  429.7 1.2 multiply_reduce_fusion
  430.9 0.9 multiply_multiply_fusion
  (38 shorter events, 1.3 us)
Async XLA Ops:
  7.2 1.6 copy-start
  7.2 32.0 %reduce-scatter.3.cloned.1.call-start = ((), (), s32[]{:S(2)}) async-start(), calls=%async_computation.2 | async-start | bytes 1310720 | tf_op jit(solution)/shard_map/reduce_scatter | solution.py:52
  11.4 113.0 %all-gather.2.cloned.1.call-start = ((), (), s32[]{:S(2)}) async-start(), calls=%async_computation.3 | async-start | bytes 9191424 | tf_op jit(solution)/shard_map/all_gather | solution.py:70
  44.8 384.9 %reduce-scatter.5.cloned.1.call-start = ((), (), s32[]{:S(2)}) async-start(), calls=%async_computation.4 | async-start | bytes 8650752 | tf_op jit(solution)/shard_map/reduce_scatter | solution.py:119
  255.3 176.5 %copy-start.1 = (bf16[512,2048]{1,0:T(8,128)(2,1)S(1)}, bf16[512,2048]{1,0:T(8,128)(2,1)}, u32[]{:S(2)}) copy-start(bf16[512,2048]{1,0:T(8,128)(2,1)} %param.10) | copy-start | bytes 6291460
  282.0 147.7 %copy-start.2 = (bf16[64,2048]{1,0:T(8,128)(2,1)S(1)}, bf16[64,2048]{1,0:T(8,128)(2,1)}, u32[]{:S(2)}) copy-start(bf16[64,2048]{1,0:T(8,128)(2,1)} %param.11) | copy-start | bytes 786436
  282.0 147.7 %copy-start.3 = (bf16[64,2048]{1,0:T(8,128)(2,1)S(1)}, bf16[64,2048]{1,0:T(8,128)(2,1)}, u32[]{:S(2)}) copy-start(bf16[64,2048]{1,0:T(8,128)(2,1)} %reduce-scatter.3.cloned.1.call-done) | copy-start | bytes 786436
  282.0 148.9 %copy-start.5 = (f32[2048]{0:T(1024)S(1)}, f32[2048]{0:T(1024)}, u32[]{:S(2)}) copy-start(f32[2048]{0:T(1024)} %param.17) | copy-start | bytes 24580
  430.9 1.0 copy-start.4
Sparse Core Ops, SparseCore 0:
  11.6 27.5 reduce-scatter.2
  44.9 79.5 all-gather.1
  282.1 147.4 reduce-scatter.4

commit v5 on v4

--- a/solution.py
+++ b/solution.py
@@ -115,10 +115,9 @@
         ) + jnp.einsum(
             "busr,bsrd->bud", weight_lo, partial_value, preferred_element_type=jnp.float32
         )
-        token_sum = combined.astype(jnp.bfloat16).reshape(-1, model_width)
-        moe_sum = lax.psum_scatter(
-            token_sum, ("expert", "tensor"), scatter_dimension=0, tiled=True
-        ).astype(jnp.float32)
+        token_sum = combined.reshape(holders, groups * row_count, model_width)
+        moe_sum = lax.psum_scatter(token_sum, "expert", scatter_dimension=0, tiled=False)
+        moe_sum = lax.psum_scatter(moe_sum, "tensor", scatter_dimension=0, tiled=True)
     else:
         expert_sum = lax.psum_scatter(partial_value, "tensor", scatter_dimension=1, tiled=True)
         returned = lax.all_to_all(expert_sum, "expert", split_axis=0, concat_axis=0, tiled=True)

time: 439 us -> 608 us (1.38)
  waiting for transfers between devices: 251 us -> 418 us
    reduce_scatter x1 -> x2, waiting for transfers between devices: 148 us -> 314 us  [the longest x1 281 us: on_device(): lax.psum_scatter(token_sum, 'expert', scatter_dimension=0, tiled=False)]
  transfers between devices with their start and end apart: 3 -> 4, of which waited for: 3 -> 4; matrix products, arithmetic and copies ran while one was open for 1% -> 1% of each run, Pallas kernels for 0% -> 0%
where the time goes in v5:
time: 608 us; the launch traced here: 607 us
  waiting for transfers between devices  418 us (69%)
  matrix products  149 us (25%)
  other arithmetic  22.8 us (4%)
  between operations  14 us (2%)
    reduce_scatter x1, waiting for transfers between devices, on_device(): lax.psum_scatter(token_sum, 'expert', scatter_dimension=0, tiled=False)  281 us
    all_gather x1, waiting for transfers between devices, on_device(): lax.all_gather(jnp.concatenate([normed, side], axis=1), ('expert', 'tenso...  76.7 us
    reduce_scatter x1, waiting for transfers between devices, on_device(): lax.psum_scatter(moe_sum, 'tensor', scatter_dimension=0, tiled=True)  32.9 us
    dot_general x1, matrix products, on_device(): jnp.einsum('busr,bsrd->bud', weight_hi, partial_value, preferred_element_...  28.9 us
    dot_general x1, matrix products, expert_partial(): jnp.einsum('nqsmd,sdf->nqsmf', block_rows, weights[:, 0], preferred_eleme...  27.7 us
    dot_general x1, matrix products, expert_partial(): jnp.einsum('nqsmd,sdf->nqsmf', block_rows, weights[:, 1], preferred_eleme...  27 us
    reduce_scatter x1, waiting for transfers between devices, on_device(): lax.psum_scatter(jnp.dot(context, out_proj, preferred_element_type=jnp.fl...  26.8 us
    dot_general x1, matrix products, on_device(): jnp.einsum('busr,bsrd->bud', weight_lo, partial_value, preferred_element_...  25.3 us
  transfers between devices with their start and end apart: 4, of which 4 were waited for; matrix products, arithmetic and copies ran while one was open for 1% of the time, Pallas kernels for 0%

profile of v5, /device:TPU:0, one launch (start us, length us, event | category | flops | bytes accessed | tf_op | source)
XLA Modules:
  0.0 607.4 jit_solution(3802967463008547198)
XLA Ops:
  7.2 1.5 copy-done
  8.8 2.7 convolution_convert_fusion.2
  11.5 0.8 fusion.82
  12.3 26.8 %reduce-scatter.4.cloned.1.call-done = bf16[64,2048]{1,0:T(8,128)(2,1)} async-done(((bf16[256,2048]{1,0:T(8,128)(2,1)}), bf16[64,2048]{1,0:T(8,128)(2,1)}) %reduce-scatter.4.cloned.1.call-update) | async-done | bytes 262160 | tf_op jit(solution)/shard_map/reduce_scatter | solution.py:52
  39.2 1.2 multiply_reduce_fusion.1
  40.4 1.9 fusion.57
  42.3 0.2 select_reduce_fusion.1
  42.9 1.2 fusion.58
  44.0 0.7 fusion.59
  44.8 0.7 fusion.67
  45.5 0.3 reduce_window_sum.11
  45.8 0.8 fusion.66
  46.8 0.3 select_reduce_fusion
  47.2 0.6 gather_fusion
  47.8 76.7 %all-gather.2.cloned.1.call-done = bf16[2048,2176]{1,0:T(8,128)(2,1)} async-done(((bf16[64,2176]{1,0:T(8,128)(2,1)}), bf16[2048,2176]{1,0:T(8,128)(2,1)}) %all-gather.2.cloned.1.call-update) | async-done | bytes 8912912 | tf_op jit(solution)/shard_map/all_gather | solution.py:70
  124.5 2.1 fusion.83
  126.6 3.7 fusion.20
  130.3 0.4 copy.70
  130.8 8.1 %fusion.31 = (bf16[32,64,64]{2,1,0:T(8,128)(2,1)S(1)}, bf16[32,64,64]{2,1,0:T(8,128)(2,1)S(1)}) fusion(s32[32,64,8]{2,1,0:T(8,128)S(1)} %get-tuple-element.10, bf16[32,64,8]{2,1,0:T(8,128)(2,1)S(1)} %get-tuple-element.9, bf16[32,64,8]{2,1,0:T(8,128)(2,1)S(1)} %get-tuple-element.8), kind=kLoop, calls=%fused_computation.33 | loop fusion | flops 4980736 | bytes 655360 | tf_op jit(solution)/shard_map/reduce_sum | solution.py:90
  138.9 0.3 copy.71
  139.3 0.3 copy.72
  139.6 0.6 fusion.49
  140.7 13.4 %convolution_convert_fusion.1 = bf16[32,16,10,2048]{3,1,2,0:T(8,128)(2,1)} fusion(bf16[32,64,2176]{2,1,0:T(8,128)(2,1)} %bitcast.103, f32[32,64,16]{1,2,0:T(8,128)S(1)} %get-tuple-element.13, f32[32,64,16]{1,2,0:T(8,128)S(1)} %copy.74), kind=kOutput, calls=%fused_computation.13 | convolution fusion | flops 1353318400 | bytes 29622272 | tf_op jit(solution)/shard_map/busr,bud->bsrd/dot_general | solution.py:105
  154.1 27.0 %fusion = f32[16,8,4,10,256]{4,3,2,1,0:T(8,128)} fusion(bf16[8,4,16,10,2048]{4,2,3,1,0:T(8,128)(2,1)} %bitcast.100, bf16[16,3,2048,256]{3,2,1,0:T(8,128)(2,1)} %param.16), kind=kOutput, calls=%fused_computation.1 | convolution fusion | flops 5368709120 | bytes 42991616 | tf_op jit(solution)/shard_map/nqsmd,sdf->nqsmf/dot_general | solution.py:18
  181.1 27.7 %fusion.14.clone.5 = bf16[8,4,16,10,256]{4,3,1,0,2:T(8,128)(2,1)} fusion(f32[16,8,4,10,256]{4,3,2,1,0:T(8,128)} %fusion, bf16[16,3,2048,256]{3,2,1,0:T(8,128)(2,1)} %param.16, bf16[8,4,16,10,2048]{4,2,3,1,0:T(8,128)(2,1)} %bitcast.101), kind=kOutput, calls=%fused_computation.20.clone.clone.clone.2 | convolution fusion | flops 5376573440 | bytes 48758784 | tf_op jit(solution)/shard_map/nqsmd,sdf->nqsmf/dot_general | solution.py:15
  208.8 21.2 %convolution_convert_fusion = bf16[16,8,4,10,2048]{4,3,2,1,0:T(8,128)(2,1)} fusion(bf16[16,3,2048,256]{3,2,1,0:T(8,128)(2,1)} %param.16, bf16[8,4,16,10,256]{4,3,1,0,2:T(8,128)(2,1)} %fusion.14.clone.5), kind=kOutput, calls=%fused_computation.5 | convolution fusion | flops 5379194880 | bytes 41943040 | tf_op jit(solution)/shard_map/nqsmf,sdf->nqsmd/dot_general | solution.py:22
  230.0 25.3 %fusion.10 = f32[32,64,2048,1]{2,1,3,0:T(8,128)} fusion(bf16[32,16,10,2048]{3,2,0,1:T(8,128)(2,1)} %bitcast.97, f32[32,64,16]{1,2,0:T(8,128)S(1)} %get-tuple-element.12, f32[32,64,16]{1,2,0:T(8,128)S(1)} %get-tuple-element.13, f32[32,64,16]{1,2,0:T(8,128)S(1)} %copy.74), kind=kOutput, calls=%fused_computation.14 | convolution fusion | flops 1343488000 | bytes 38141952 | tf_op jit(solution)/shard_map/busr,bsrd->bud/dot_general | solution.py:115
  255.3 28.9 %bitcast_add_fusion = f32[32,64,2048]{2,1,0:T(8,128)} fusion(f32[32,64,2048,1]{2,1,3,0:T(8,128)} %fusion.10, bf16[32,16,10,2048]{3,2,0,1:T(8,128)(2,1)} %bitcast.98, f32[32,64,16]{1,2,0:T(8,128)S(1)} %get-tuple-element.11, f32[32,64,16]{1,2,0:T(8,128)S(1)} %get-tuple-element.13, f32[32,64,16]{1,2,0:T(8,128)S(1)} %copy.74), kind=kOutput, calls=%fused_computation.9 | convolution fusion | flops 1347682304 | bytes 54919168 | tf_op jit(solution)/shard_map/busr,bsrd->bud/dot_general | solution.py:113
  284.4 281.4 %reduce-scatter.6.cloned.1.call-done = f32[1,256,2048]{2,1,0:T(8,128)} async-done(((f32[8,256,2048]{2,1,0:T(8,128)}), f32[1,256,2048]{2,1,0:T(8,128)}) %reduce-scatter.6.cloned.1.call-update) | async-done | bytes 2097168 | tf_op jit(solution)/shard_map/reduce_scatter | solution.py:119
  565.7 32.9 %reduce-scatter.8.cloned.1.call-done = f32[64,2048]{1,0:T(8,128)} async-done(((f32[256,2048]{1,0:T(8,128)}), f32[64,2048]{1,0:T(8,128)}) %reduce-scatter.8.cloned.1.call-update) | async-done | bytes 524304 | tf_op jit(solution)/shard_map/reduce_scatter | solution.py:120
  598.6 1.2 multiply_reduce_fusion
  599.9 0.9 multiply_multiply_fusion
  (41 shorter events, 1.5 us)
Async XLA Ops:
  7.2 1.6 copy-start
  7.2 32.0 %reduce-scatter.4.cloned.1.call-start = ((), (), s32[]{:S(2)}) async-start(), calls=%async_computation.3 | async-start | bytes 1310720 | tf_op jit(solution)/shard_map/reduce_scatter | solution.py:52
  11.4 113.0 %all-gather.2.cloned.1.call-start = ((), (), s32[]{:S(2)}) async-start(), calls=%async_computation.4 | async-start | bytes 9191424 | tf_op jit(solution)/shard_map/all_gather | solution.py:70
  44.8 520.9 %reduce-scatter.6.cloned.1.call-start = ((), (), s32[]{:S(2)}) async-start(), calls=%async_computation.5 | async-start | bytes 18874368 | tf_op jit(solution)/shard_map/reduce_scatter | solution.py:119
  284.3 316.6 %copy-start.1 = (bf16[512,2048]{1,0:T(8,128)(2,1)S(1)}, bf16[512,2048]{1,0:T(8,128)(2,1)}, u32[]{:S(2)}) copy-start(bf16[512,2048]{1,0:T(8,128)(2,1)} %param.10) | copy-start | bytes 6291460
  284.3 314.3 %copy-start.2 = (bf16[64,2048]{1,0:T(8,128)(2,1)S(1)}, bf16[64,2048]{1,0:T(8,128)(2,1)}, u32[]{:S(2)}) copy-start(bf16[64,2048]{1,0:T(8,128)(2,1)} %param.11) | copy-start | bytes 786436
  284.3 314.3 %copy-start.3 = (bf16[64,2048]{1,0:T(8,128)(2,1)S(1)}, bf16[64,2048]{1,0:T(8,128)(2,1)}, u32[]{:S(2)}) copy-start(bf16[64,2048]{1,0:T(8,128)(2,1)} %reduce-scatter.4.cloned.1.call-done) | copy-start | bytes 786436
  284.3 315.6 %copy-start.5 = (f32[2048]{0:T(1024)S(1)}, f32[2048]{0:T(1024)}, u32[]{:S(2)}) copy-start(f32[2048]{0:T(1024)} %param.17) | copy-start | bytes 24580
  284.3 314.3 %reduce-scatter.8.cloned.1.call-start = ((), (), s32[]{:S(2)}) async-start(), calls=%async_computation.6 | async-start | bytes 2621440 | tf_op jit(solution)/shard_map/reduce_scatter | solution.py:120
  599.8 1.0 copy-start.4
Sparse Core Ops, SparseCore 0:
  11.6 27.5 reduce-scatter.3
  44.9 79.5 all-gather.1
  284.4 281.2 reduce-scatter.5
  568.1 30.4 reduce-scatter.7

commit v6 on v4

--- a/solution.py
+++ b/solution.py
@@ -11,14 +11,14 @@
     return values * lax.rsqrt(mean_square + EPS) * gain_row
 
 
-def expert_partial(block_rows, weights):
-    gate_pre = jnp.einsum(
-        "nqsmd,sdf->nqsmf", block_rows, weights[:, 0], preferred_element_type=jnp.float32
+def expert_inner(block_rows, weights):
+    both_pre = jnp.einsum(
+        "nqsmd,scdf->nqsmcf", block_rows, weights[:, :2], preferred_element_type=jnp.float32
     )
-    up_pre = jnp.einsum(
-        "nqsmd,sdf->nqsmf", block_rows, weights[:, 1], preferred_element_type=jnp.float32
-    )
-    inner_act = (jax.nn.silu(gate_pre) * up_pre).astype(jnp.bfloat16)
+    return jax.nn.silu(both_pre[..., 0, :]) * both_pre[..., 1, :]
+
+
+def expert_down(inner_act, weights):
     return jnp.einsum(
         "nqsmf,sdf->nqsmd", inner_act, weights[:, 2], preferred_element_type=jnp.float32
     )
@@ -105,21 +105,25 @@
     received = jnp.einsum(
         "busr,bud->bsrd", pick_hot, all_rows, preferred_element_type=jnp.float32
     ).astype(jnp.bfloat16).reshape(holders, groups, slot_dev, capacity, model_width)
-    partial_value = expert_partial(received, expert_weights).astype(jnp.bfloat16)
+    inner_f32 = expert_inner(received, expert_weights)
     if blocks * row_count * model_width * 4 <= (32 << 20):
+        gate_sel = gate_sel_hi + gate_sel_lo
+        pair_gate = jnp.sum(pick * gate_sel[..., None], axis=1)
+        pair_gate = pair_gate.reshape(holders, groups, slot_dev, capacity, 1)
+        inner_act = (inner_f32 * pair_gate).astype(jnp.bfloat16)
+        partial_value = expert_down(inner_act, expert_weights).astype(jnp.bfloat16)
         partial_value = partial_value.reshape(blocks, slot_dev, capacity, model_width)
-        weight_hi = (pick * gate_sel_hi[..., None]).astype(jnp.bfloat16)
-        weight_lo = (pick * gate_sel_lo[..., None]).astype(jnp.bfloat16)
         combined = jnp.einsum(
-            "busr,bsrd->bud", weight_hi, partial_value, preferred_element_type=jnp.float32
-        ) + jnp.einsum(
-            "busr,bsrd->bud", weight_lo, partial_value, preferred_element_type=jnp.float32
+            "busr,bsrd->bud", pick_hot, partial_value, preferred_element_type=jnp.float32
         )
         token_sum = combined.astype(jnp.bfloat16).reshape(-1, model_width)
         moe_sum = lax.psum_scatter(
             token_sum, ("expert", "tensor"), scatter_dimension=0, tiled=True
         ).astype(jnp.float32)
     else:
+        partial_value = expert_down(
+            inner_f32.astype(jnp.bfloat16), expert_weights
+        ).astype(jnp.bfloat16)
         expert_sum = lax.psum_scatter(partial_value, "tensor", scatter_dimension=1, tiled=True)
         returned = lax.all_to_all(expert_sum, "expert", split_axis=0, concat_axis=0, tiled=True)
         own_flat = own_ids.reshape(-1)

time: 439 us -> 407 us (0.927)
  matrix products: 147 us -> 114 us
    dot_general x5 -> x3, matrix products: 128 us -> 95.5 us  [the longest x1 46.3 us: expert_inner(): jnp.einsum('nqsmd,scdf->nqsmcf', block_rows, weights[:, :2], preferred_el...]
where the time goes in v6:
time: 407 us
  waiting for transfers between devices  251 us (62%)
  matrix products  114 us (28%)
  other arithmetic  23.4 us (6%)
  between operations  14 us (3%)
    reduce_scatter x1, waiting for transfers between devices, on_device(): lax.psum_scatter(token_sum, ('expert', 'tensor'), scatter_dimension=0, ti...  148 us
    all_gather x1, waiting for transfers between devices, on_device(): lax.all_gather(jnp.concatenate([normed, side], axis=1), ('expert', 'tenso...  76.7 us
    dot_general x1, matrix products, expert_inner(): jnp.einsum('nqsmd,scdf->nqsmcf', block_rows, weights[:, :2], preferred_el...  46.3 us
    reduce_scatter x1, waiting for transfers between devices, on_device(): lax.psum_scatter(jnp.dot(context, out_proj, preferred_element_type=jnp.fl...  26.8 us
    dot_general x1, matrix products, on_device(): jnp.einsum('busr,bsrd->bud', pick_hot, partial_value, preferred_element_t...  25.8 us
    dot_general x1, matrix products, expert_down(): jnp.einsum('nqsmf,sdf->nqsmd', inner_act, weights[:, 2], preferred_elemen...  23.3 us
    dot_general x1, matrix products, on_device(): jnp.einsum('busr,bud->bsrd', pick_hot, all_rows, preferred_element_type=j...  13.4 us
  transfers between devices with their start and end apart: 3, of which 3 were waited for; matrix products, arithmetic and copies ran while one was open for 1% of the time, Pallas kernels for 0%

profile of v6, /device:TPU:0, one launch (start us, length us, event | category | flops | bytes accessed | tf_op | source)
XLA Modules:
  0.0 406.8 jit_solution(15297157783352293599)
XLA Ops:
  7.2 1.5 copy-done
  8.8 2.7 convolution_convert_fusion.2
  11.5 0.8 fusion.63
  12.3 26.8 %reduce-scatter.3.cloned.1.call-done = bf16[64,2048]{1,0:T(8,128)(2,1)} async-done(((bf16[256,2048]{1,0:T(8,128)(2,1)}), bf16[64,2048]{1,0:T(8,128)(2,1)}) %reduce-scatter.3.cloned.1.call-update) | async-done | bytes 262160 | tf_op jit(solution)/shard_map/reduce_scatter | solution.py:52
  39.2 1.2 multiply_reduce_fusion.1
  40.4 1.9 fusion.40
  42.3 0.2 select_reduce_fusion.1
  42.9 1.2 fusion.41
  44.0 0.7 fusion.42
  44.8 0.7 fusion.50
  45.5 0.3 reduce_window_sum.11
  45.8 0.8 fusion.49
  46.8 0.3 select_reduce_fusion
  47.2 0.6 gather_fusion
  47.8 76.7 %all-gather.2.cloned.1.call-done = bf16[2048,2176]{1,0:T(8,128)(2,1)} async-done(((bf16[64,2176]{1,0:T(8,128)(2,1)}), bf16[2048,2176]{1,0:T(8,128)(2,1)}) %all-gather.2.cloned.1.call-update) | async-done | bytes 8912912 | tf_op jit(solution)/shard_map/all_gather | solution.py:70
  124.5 2.1 fusion.64
  126.6 3.5 fusion.18
  130.2 0.4 copy.62
  130.6 8.1 %fusion.21 = (bf16[32,64,64]{2,1,0:T(8,128)(2,1)S(1)}, bf16[32,64,64]{2,1,0:T(8,128)(2,1)S(1)}) fusion(s32[32,64,8]{2,1,0:T(8,128)S(1)} %get-tuple-element.10, bf16[32,64,8]{2,1,0:T(8,128)(2,1)S(1)} %get-tuple-element.9, bf16[32,64,8]{2,1,0:T(8,128)(2,1)S(1)} %get-tuple-element.8), kind=kLoop, calls=%fused_computation.23 | loop fusion | flops 4980736 | bytes 655360 | tf_op jit(solution)/shard_map/reduce_sum | solution.py:90
  138.7 0.3 copy.63
  139.1 0.3 copy.64
  139.4 0.6 fusion.33
  140.2 0.2 convolution_bitcast_fusion
  140.6 13.4 %convolution_convert_fusion.1 = bf16[32,16,10,2048]{3,1,2,0:T(8,128)(2,1)} fusion(bf16[32,64,2176]{2,1,0:T(8,128)(2,1)} %bitcast.75, f32[32,64,16]{1,2,0:T(8,128)S(1)} %get-tuple-element.12, f32[32,64,16]{1,2,0:T(8,128)S(1)} %copy.66), kind=kOutput, calls=%fused_computation.11 | convolution fusion | flops 1353318400 | bytes 29622272 | tf_op jit(solution)/shard_map/busr,bud->bsrd/dot_general | solution.py:105
  153.9 0.8 fusion.26
  154.7 0.4 copy.69
  155.1 46.3 %fusion.8 = f32[8,4,16,10,2,256]{5,3,4,1,0,2:T(8,128)} fusion(bf16[16,3,2048,256]{3,2,1,0:T(8,128)(2,1)} %param.16, bf16[8,4,16,10,2048,1]{4,2,3,1,0,5:T(8,128)(2,1)} %bitcast.72), kind=kOutput, calls=%fused_computation.12 | convolution fusion | flops 10737418240 | bytes 65011712 | tf_op jit(solution)/shard_map/nqsmd,scdf->nqsmcf/dot_general | solution.py:15
  201.4 23.3 %convolution_convert_fusion = bf16[16,8,4,10,2048]{4,3,2,1,0:T(8,128)(2,1)} fusion(bf16[16,3,2048,256]{3,2,1,0:T(8,128)(2,1)} %param.16, f32[8,4,16,10,2,256]{5,3,4,1,0,2:T(8,128)} %fusion.8, f32[8,4,16,10]{3,1,0,2:T(4,128)S(1)} %copy.69), kind=kOutput, calls=%fused_computation.7 | convolution fusion | flops 5388369920 | bytes 54546432 | tf_op jit(solution)/shard_map/nqsmf,sdf->nqsmd/dot_general | solution.py:22
  224.8 25.8 %bitcast_convert_fusion = bf16[32,64,2048]{2,1,0:T(8,128)(2,1)} fusion(bf16[32,16,10,2048]{3,2,0,1:T(8,128)(2,1)} %bitcast.73, f32[32,64,16]{1,2,0:T(8,128)S(1)} %get-tuple-element.12, f32[32,64,16]{1,2,0:T(8,128)S(1)} %copy.66), kind=kOutput, calls=%fused_computation.9 | convolution fusion | flops 1347026944 | bytes 29622272 | tf_op jit(solution)/shard_map/busr,bsrd->bud/dot_general | solution.py:116
  250.6 147.6 %reduce-scatter.5.cloned.1.call-done = bf16[64,2048]{1,0:T(8,128)(2,1)} async-done(((bf16[2048,2048]{1,0:T(8,128)(2,1)}), bf16[64,2048]{1,0:T(8,128)(2,1)}) %reduce-scatter.5.cloned.1.call-update) | async-done | bytes 262160 | tf_op jit(solution)/shard_map/reduce_scatter | solution.py:120
  398.1 1.2 multiply_reduce_fusion
  399.4 0.9 multiply_multiply_fusion
  (38 shorter events, 1.3 us)
Async XLA Ops:
  7.2 1.6 copy-start
  7.2 32.0 %reduce-scatter.3.cloned.1.call-start = ((), (), s32[]{:S(2)}) async-start(), calls=%async_computation.2 | async-start | bytes 1310720 | tf_op jit(solution)/shard_map/reduce_scatter | solution.py:52
  11.4 113.0 %all-gather.2.cloned.1.call-start = ((), (), s32[]{:S(2)}) async-start(), calls=%async_computation.3 | async-start | bytes 9191424 | tf_op jit(solution)/shard_map/all_gather | solution.py:70
  44.8 353.4 %reduce-scatter.5.cloned.1.call-start = ((), (), s32[]{:S(2)}) async-start(), calls=%async_computation.4 | async-start | bytes 8650752 | tf_op jit(solution)/shard_map/reduce_scatter | solution.py:120
  224.7 175.6 %copy-start.1 = (bf16[512,2048]{1,0:T(8,128)(2,1)S(1)}, bf16[512,2048]{1,0:T(8,128)(2,1)}, u32[]{:S(2)}) copy-start(bf16[512,2048]{1,0:T(8,128)(2,1)} %param.10) | copy-start | bytes 6291460
  250.5 147.6 %copy-start.2 = (bf16[64,2048]{1,0:T(8,128)(2,1)S(1)}, bf16[64,2048]{1,0:T(8,128)(2,1)}, u32[]{:S(2)}) copy-start(bf16[64,2048]{1,0:T(8,128)(2,1)} %param.11) | copy-start | bytes 786436
  250.5 147.6 %copy-start.3 = (bf16[64,2048]{1,0:T(8,128)(2,1)S(1)}, bf16[64,2048]{1,0:T(8,128)(2,1)}, u32[]{:S(2)}) copy-start(bf16[64,2048]{1,0:T(8,128)(2,1)} %reduce-scatter.3.cloned.1.call-done) | copy-start | bytes 786436
  250.5 148.8 %copy-start.5 = (f32[2048]{0:T(1024)S(1)}, f32[2048]{0:T(1024)}, u32[]{:S(2)}) copy-start(f32[2048]{0:T(1024)} %param.17) | copy-start | bytes 24580
  399.3 1.0 copy-start.4
Sparse Core Ops, SparseCore 0:
  11.6 27.5 reduce-scatter.2
  44.9 79.5 all-gather.1
  250.7 147.4 reduce-scatter.4

commit v7 on v6

--- a/solution.py
+++ b/solution.py
@@ -116,9 +116,10 @@
         combined = jnp.einsum(
             "busr,bsrd->bud", pick_hot, partial_value, preferred_element_type=jnp.float32
         )
-        token_sum = combined.astype(jnp.bfloat16).reshape(-1, model_width)
+        token_sum = combined.astype(jnp.bfloat16).reshape(holders, groups, row_count, model_width)
+        moe_sum = lax.psum_scatter(token_sum, "tensor", scatter_dimension=1, tiled=False)
         moe_sum = lax.psum_scatter(
-            token_sum, ("expert", "tensor"), scatter_dimension=0, tiled=True
+            moe_sum, "expert", scatter_dimension=0, tiled=False
         ).astype(jnp.float32)
     else:
         partial_value = expert_down(

time: 407 us -> 410 us (level)
  local copies, waits for them, and re-layouts: 3.95 us -> 12.4 us
  waiting for transfers between devices: 251 us -> 246 us
    reshape x0 -> x1, local copies, waits for them, and re-layouts: none -> 8.41 us  [on_device(): combined.astype(jnp.bfloat16)]
    reduce_scatter x1 -> x2, waiting for transfers between devices: 148 us -> 142 us  [the longest x1 71.5 us: on_device(): lax.psum_scatter(moe_sum, 'expert', scatter_dimension=0, tiled=False)]
  transfers between devices with their start and end apart: 3 -> 4, of which waited for: 3 -> 4; matrix products, arithmetic and copies ran while one was open for 1% -> 1% of each run, Pallas kernels for 0% -> 0%
where the time goes in v7:
time: 410 us
  waiting for transfers between devices  246 us (60%)
  matrix products  114 us (28%)
  other arithmetic  23.4 us (6%)
  between operations  14 us (3%)
  local copies, waits for them, and re-layouts  12.4 us (3%)
    all_gather x1, waiting for transfers between devices, on_device(): lax.all_gather(jnp.concatenate([normed, side], axis=1), ('expert', 'tenso...  76.7 us
    reduce_scatter x1, waiting for transfers between devices, on_device(): lax.psum_scatter(moe_sum, 'expert', scatter_dimension=0, tiled=False)  71.5 us
    reduce_scatter x1, waiting for transfers between devices, on_device(): lax.psum_scatter(token_sum, 'tensor', scatter_dimension=1, tiled=False)  70.4 us
    dot_general x1, matrix products, expert_inner(): jnp.einsum('nqsmd,scdf->nqsmcf', block_rows, weights[:, :2], preferred_el...  46.3 us
    reduce_scatter x1, waiting for transfers between devices, on_device(): lax.psum_scatter(jnp.dot(context, out_proj, preferred_element_type=jnp.fl...  26.8 us
    dot_general x1, matrix products, on_device(): jnp.einsum('busr,bsrd->bud', pick_hot, partial_value, preferred_element_t...  25.6 us
    dot_general x1, matrix products, expert_down(): jnp.einsum('nqsmf,sdf->nqsmd', inner_act, weights[:, 2], preferred_elemen...  23.3 us
    dot_general x1, matrix products, on_device(): jnp.einsum('busr,bud->bsrd', pick_hot, all_rows, preferred_element_type=j...  13.4 us
  transfers between devices with their start and end apart: 4, of which 4 were waited for; matrix products, arithmetic and copies ran while one was open for 1% of the time, Pallas kernels for 0%

profile of v7, /device:TPU:0, one launch (start us, length us, event | category | flops | bytes accessed | tf_op | source)
XLA Modules:
  0.0 409.5 jit_solution(13442242095821888340)
XLA Ops:
  7.2 1.5 copy-done
  8.8 2.7 convolution_convert_fusion.2
  11.5 0.8 fusion.63
  12.3 26.8 %reduce-scatter.4.cloned.1.call-done = bf16[64,2048]{1,0:T(8,128)(2,1)} async-done(((bf16[256,2048]{1,0:T(8,128)(2,1)}), bf16[64,2048]{1,0:T(8,128)(2,1)}) %reduce-scatter.4.cloned.1.call-update) | async-done | bytes 262160 | tf_op jit(solution)/shard_map/reduce_scatter | solution.py:52
  39.2 1.2 multiply_reduce_fusion.1
  40.4 1.9 fusion.40
  42.9 1.2 fusion.41
  44.0 0.7 fusion.42
  44.8 0.7 fusion.50
  45.5 0.3 reduce_window_sum.11
  45.8 0.8 fusion.49
  46.8 0.3 select_reduce_fusion
  47.2 0.6 gather_fusion
  47.8 76.7 %all-gather.2.cloned.1.call-done = bf16[2048,2176]{1,0:T(8,128)(2,1)} async-done(((bf16[64,2176]{1,0:T(8,128)(2,1)}), bf16[2048,2176]{1,0:T(8,128)(2,1)}) %all-gather.2.cloned.1.call-update) | async-done | bytes 8912912 | tf_op jit(solution)/shard_map/all_gather | solution.py:70
  124.5 2.1 fusion.64
  126.6 3.5 fusion.18
  130.2 0.4 copy.66
  130.6 8.1 %fusion.21 = (bf16[32,64,64]{2,1,0:T(8,128)(2,1)S(1)}, bf16[32,64,64]{2,1,0:T(8,128)(2,1)S(1)}) fusion(s32[32,64,8]{2,1,0:T(8,128)S(1)} %get-tuple-element.10, bf16[32,64,8]{2,1,0:T(8,128)(2,1)S(1)} %get-tuple-element.9, bf16[32,64,8]{2,1,0:T(8,128)(2,1)S(1)} %get-tuple-element.8), kind=kLoop, calls=%fused_computation.23 | loop fusion | flops 4980736 | bytes 655360 | tf_op jit(solution)/shard_map/reduce_sum | solution.py:90
  138.7 0.3 copy.67
  139.1 0.3 copy.68
  139.4 0.6 fusion.33
  140.6 13.4 %convolution_convert_fusion.1 = bf16[32,16,10,2048]{3,1,2,0:T(8,128)(2,1)} fusion(bf16[32,64,2176]{2,1,0:T(8,128)(2,1)} %bitcast.80, f32[32,64,16]{1,2,0:T(8,128)S(1)} %get-tuple-element.12, f32[32,64,16]{1,2,0:T(8,128)S(1)} %copy.70), kind=kOutput, calls=%fused_computation.11 | convolution fusion | flops 1353318400 | bytes 29622272 | tf_op jit(solution)/shard_map/busr,bud->bsrd/dot_general | solution.py:105
  153.9 0.8 fusion.26
  154.7 0.4 copy.73
  155.1 46.3 %fusion.8 = f32[8,4,16,10,2,256]{5,3,4,1,0,2:T(8,128)} fusion(bf16[16,3,2048,256]{3,2,1,0:T(8,128)(2,1)} %param.16, bf16[8,4,16,10,2048,1]{4,2,3,1,0,5:T(8,128)(2,1)} %bitcast.77), kind=kOutput, calls=%fused_computation.12 | convolution fusion | flops 10737418240 | bytes 65011712 | tf_op jit(solution)/shard_map/nqsmd,scdf->nqsmcf/dot_general | solution.py:15
  201.4 23.3 %convolution_convert_fusion = bf16[16,8,4,10,2048]{4,3,2,1,0:T(8,128)(2,1)} fusion(bf16[16,3,2048,256]{3,2,1,0:T(8,128)(2,1)} %param.16, f32[8,4,16,10,2,256]{5,3,4,1,0,2:T(8,128)} %fusion.8, f32[8,4,16,10]{3,1,0,2:T(4,128)S(1)} %copy.73), kind=kOutput, calls=%fused_computation.7 | convolution fusion | flops 5388369920 | bytes 54546432 | tf_op jit(solution)/shard_map/nqsmf,sdf->nqsmd/dot_general | solution.py:22
  224.7 25.6 %bitcast_convert_fusion = bf16[32,64,2048]{2,1,0:T(8,128)(2,1)} fusion(bf16[32,16,10,2048]{3,2,0,1:T(8,128)(2,1)} %bitcast.78, f32[32,64,16]{1,2,0:T(8,128)S(1)} %get-tuple-element.12, f32[32,64,16]{1,2,0:T(8,128)S(1)} %copy.70), kind=kOutput, calls=%fused_computation.9 | convolution fusion | flops 1347026944 | bytes 29622272 | tf_op jit(solution)/shard_map/busr,bsrd->bud/dot_general | solution.py:116
  250.4 8.4 %copy.76 = bf16[8,4,64,2048]{3,2,0,1:T(8,128)(2,1)} copy(bf16[8,4,64,2048]{3,2,1,0:T(8,128)(2,1)} %bitcast.76) | data formatting | bytes 16777216 | tf_op jit(solution)/shard_map/reshape | solution.py:119
  258.9 70.4 %reduce-scatter.6.cloned.1.call-done = bf16[8,1,64,2048]{3,2,0,1:T(8,128)(2,1)} async-done(((bf16[8,4,64,2048]{3,2,0,1:T(8,128)(2,1)}), bf16[8,1,64,2048]{3,2,0,1:T(8,128)(2,1)}) %reduce-scatter.6.cloned.1.call-update) | async-done | bytes 2097168 | tf_op jit(solution)/shard_map/reduce_scatter | solution.py:120
  329.3 71.5 %reduce-scatter.8.cloned.1.call-done = bf16[1,64,2048]{2,1,0:T(8,128)(2,1)} async-done(((bf16[8,64,2048]{2,1,0:T(8,128)(2,1)}), bf16[1,64,2048]{2,1,0:T(8,128)(2,1)}) %reduce-scatter.8.cloned.1.call-update) | async-done | bytes 262160 | tf_op jit(solution)/shard_map/reduce_scatter | solution.py:121
  400.8 1.2 multiply_reduce_fusion
  402.1 0.9 multiply_multiply_fusion
  (42 shorter events, 1.8 us)
Async XLA Ops:
  7.2 1.6 copy-start
  7.2 32.0 %reduce-scatter.4.cloned.1.call-start = ((), (), s32[]{:S(2)}) async-start(), calls=%async_computation.3 | async-start | bytes 1310720 | tf_op jit(solution)/shard_map/reduce_scatter | solution.py:52
  11.4 113.0 %all-gather.2.cloned.1.call-start = ((), (), s32[]{:S(2)}) async-start(), calls=%async_computation.4 | async-start | bytes 9191424 | tf_op jit(solution)/shard_map/all_gather | solution.py:70
  44.8 284.5 %reduce-scatter.6.cloned.1.call-start = ((), (), s32[]{:S(2)}) async-start(), calls=%async_computation.5 | async-start | bytes 10485760 | tf_op jit(solution)/shard_map/reduce_scatter | solution.py:120
  250.4 152.6 %copy-start.1 = (bf16[512,2048]{1,0:T(8,128)(2,1)S(1)}, bf16[512,2048]{1,0:T(8,128)(2,1)}, u32[]{:S(2)}) copy-start(bf16[512,2048]{1,0:T(8,128)(2,1)} %param.10) | copy-start | bytes 6291460
  258.8 142.0 %copy-start.2 = (bf16[64,2048]{1,0:T(8,128)(2,1)S(1)}, bf16[64,2048]{1,0:T(8,128)(2,1)}, u32[]{:S(2)}) copy-start(bf16[64,2048]{1,0:T(8,128)(2,1)} %param.11) | copy-start | bytes 786436
  258.8 142.0 %copy-start.3 = (bf16[64,2048]{1,0:T(8,128)(2,1)S(1)}, bf16[64,2048]{1,0:T(8,128)(2,1)}, u32[]{:S(2)}) copy-start(bf16[64,2048]{1,0:T(8,128)(2,1)} %reduce-scatter.4.cloned.1.call-done) | copy-start | bytes 786436
  258.8 143.2 %copy-start.5 = (f32[2048]{0:T(1024)S(1)}, f32[2048]{0:T(1024)}, u32[]{:S(2)}) copy-start(f32[2048]{0:T(1024)} %param.17) | copy-start | bytes 24580
  258.8 142.0 %reduce-scatter.8.cloned.1.call-start = ((), (), s32[]{:S(2)}) async-start(), calls=%async_computation.6 | async-start | bytes 2359296 | tf_op jit(solution)/shard_map/reduce_scatter | solution.py:121
  402.0 1.0 copy-start.4
Sparse Core Ops, SparseCore 0:
  11.6 27.5 reduce-scatter.3
  44.9 79.5 all-gather.1
  258.9 70.3 reduce-scatter.5
  332.7 68.0 reduce-scatter.7

commit v8 on v7

--- a/solution.py
+++ b/solution.py
@@ -117,10 +117,14 @@
             "busr,bsrd->bud", pick_hot, partial_value, preferred_element_type=jnp.float32
         )
         token_sum = combined.astype(jnp.bfloat16).reshape(holders, groups, row_count, model_width)
-        moe_sum = lax.psum_scatter(token_sum, "tensor", scatter_dimension=1, tiled=False)
         moe_sum = lax.psum_scatter(
-            moe_sum, "expert", scatter_dimension=0, tiled=False
-        ).astype(jnp.float32)
+            jnp.swapaxes(token_sum, 0, 1).reshape(-1, model_width),
+            "tensor",
+            scatter_dimension=0,
+            tiled=True,
+        ).reshape(holders, row_count, model_width)
+        moe_sum = lax.all_to_all(moe_sum, "expert", split_axis=0, concat_axis=0, tiled=True)
+        moe_sum = jnp.sum(moe_sum.astype(jnp.float32), axis=0)
     else:
         partial_value = expert_down(
             inner_f32.astype(jnp.bfloat16), expert_weights

time: 410 us -> 391 us (0.954)
  waiting for transfers between devices: 246 us -> 174 us
  blocking collectives: 0 us -> 53.7 us
    reduce_scatter x2 -> x1, waiting for transfers between devices: 142 us -> 70.5 us  [on_device(): lax.psum_scatter(jnp.swapaxes(token_sum, 0, 1).reshape(-1, model_width),...]
    all_to_all x0 -> x1, blocking collectives: none -> 53.7 us  [on_device(): lax.all_to_all(moe_sum, 'expert', split_axis=0, concat_axis=0, tiled=True)]
  transfers between devices with their start and end apart: 4 -> 3, of which waited for: 4 -> 3; matrix products, arithmetic and copies ran while one was open for 1% -> 1% of each run, Pallas kernels for 0% -> 0%
where the time goes in v8:
time: 391 us
  waiting for transfers between devices  174 us (45%)
  matrix products  114 us (29%)
  blocking collectives  53.7 us (14%)
  other arithmetic  22.8 us (6%)
  between operations  14 us (4%)
  local copies, waits for them, and re-layouts  12.2 us (3%)
    all_gather x1, waiting for transfers between devices, on_device(): lax.all_gather(jnp.concatenate([normed, side], axis=1), ('expert', 'tenso...  76.7 us
    reduce_scatter x1, waiting for transfers between devices, on_device(): lax.psum_scatter(jnp.swapaxes(token_sum, 0, 1).reshape(-1, model_width),...  70.5 us
    all_to_all x1, blocking collectives, on_device(): lax.all_to_all(moe_sum, 'expert', split_axis=0, concat_axis=0, tiled=True)  53.7 us
    dot_general x1, matrix products, expert_inner(): jnp.einsum('nqsmd,scdf->nqsmcf', block_rows, weights[:, :2], preferred_el...  46.3 us
    reduce_scatter x1, waiting for transfers between devices, on_device(): lax.psum_scatter(jnp.dot(context, out_proj, preferred_element_type=jnp.fl...  26.8 us
    dot_general x1, matrix products, on_device(): jnp.einsum('busr,bsrd->bud', pick_hot, partial_value, preferred_element_t...  25.6 us
    dot_general x1, matrix products, expert_down(): jnp.einsum('nqsmf,sdf->nqsmd', inner_act, weights[:, 2], preferred_elemen...  23.3 us
    dot_general x1, matrix products, on_device(): jnp.einsum('busr,bud->bsrd', pick_hot, all_rows, preferred_element_type=j...  13.4 us
  transfers between devices with their start and end apart: 3, of which 3 were waited for; matrix products, arithmetic and copies ran while one was open for 1% of the time, Pallas kernels for 0%

profile of v8, /device:TPU:0, one launch (start us, length us, event | category | flops | bytes accessed | tf_op | source)
XLA Modules:
  0.0 391.0 jit_solution(10141684109521038110)
XLA Ops:
  7.2 1.5 copy-done
  8.8 2.7 convolution_convert_fusion.2
  11.5 0.8 fusion.65
  12.3 26.8 %reduce-scatter.3.cloned.1.call-done = bf16[64,2048]{1,0:T(8,128)(2,1)} async-done(((bf16[256,2048]{1,0:T(8,128)(2,1)}), bf16[64,2048]{1,0:T(8,128)(2,1)}) %reduce-scatter.3.cloned.1.call-update) | async-done | bytes 262160 | tf_op jit(solution)/shard_map/reduce_scatter | solution.py:52
  39.2 1.2 multiply_reduce_fusion.1
  40.4 1.9 fusion.41
  42.9 1.2 fusion.42
  44.0 0.7 fusion.43
  44.8 0.7 fusion.51
  45.5 0.3 reduce_window_sum.11
  45.8 0.8 fusion.50
  46.8 0.3 select_reduce_fusion
  47.2 0.6 gather_fusion
  47.8 76.7 %all-gather.2.cloned.1.call-done = bf16[2048,2176]{1,0:T(8,128)(2,1)} async-done(((bf16[64,2176]{1,0:T(8,128)(2,1)}), bf16[2048,2176]{1,0:T(8,128)(2,1)}) %all-gather.2.cloned.1.call-update) | async-done | bytes 8912912 | tf_op jit(solution)/shard_map/all_gather | solution.py:70
  124.5 2.1 fusion.66
  126.6 3.5 fusion.18
  130.2 0.4 copy.66
  130.6 8.1 %fusion.21 = (bf16[32,64,64]{2,1,0:T(8,128)(2,1)S(1)}, bf16[32,64,64]{2,1,0:T(8,128)(2,1)S(1)}) fusion(s32[32,64,8]{2,1,0:T(8,128)S(1)} %get-tuple-element.10, bf16[32,64,8]{2,1,0:T(8,128)(2,1)S(1)} %get-tuple-element.9, bf16[32,64,8]{2,1,0:T(8,128)(2,1)S(1)} %get-tuple-element.8), kind=kLoop, calls=%fused_computation.23 | loop fusion | flops 4980736 | bytes 655360 | tf_op jit(solution)/shard_map/reduce_sum | solution.py:90
  138.7 0.3 copy.67
  139.1 0.3 copy.68
  139.4 0.6 fusion.33
  140.6 13.4 %convolution_convert_fusion.1 = bf16[32,16,10,2048]{3,1,2,0:T(8,128)(2,1)} fusion(bf16[32,64,2176]{2,1,0:T(8,128)(2,1)} %bitcast.80, f32[32,64,16]{1,2,0:T(8,128)S(1)} %get-tuple-element.12, f32[32,64,16]{1,2,0:T(8,128)S(1)} %copy.70), kind=kOutput, calls=%fused_computation.11 | convolution fusion | flops 1353318400 | bytes 29622272 | tf_op jit(solution)/shard_map/busr,bud->bsrd/dot_general | solution.py:105
  153.9 0.8 fusion.26
  154.7 0.4 copy.73
  155.1 46.3 %fusion.8 = f32[8,4,16,10,2,256]{5,3,4,1,0,2:T(8,128)} fusion(bf16[16,3,2048,256]{3,2,1,0:T(8,128)(2,1)} %param.16, bf16[8,4,16,10,2048,1]{4,2,3,1,0,5:T(8,128)(2,1)} %bitcast.76), kind=kOutput, calls=%fused_computation.12 | convolution fusion | flops 10737418240 | bytes 65011712 | tf_op jit(solution)/shard_map/nqsmd,scdf->nqsmcf/dot_general | solution.py:15
  201.4 23.3 %convolution_convert_fusion = bf16[16,8,4,10,2048]{4,3,2,1,0:T(8,128)(2,1)} fusion(bf16[16,3,2048,256]{3,2,1,0:T(8,128)(2,1)} %param.16, f32[8,4,16,10,2,256]{5,3,4,1,0,2:T(8,128)} %fusion.8, f32[8,4,16,10]{3,1,0,2:T(4,128)S(1)} %copy.73), kind=kOutput, calls=%fused_computation.7 | convolution fusion | flops 5388369920 | bytes 54546432 | tf_op jit(solution)/shard_map/nqsmf,sdf->nqsmd/dot_general | solution.py:22
  224.7 25.6 %bitcast_convert_fusion = bf16[32,64,2048]{2,1,0:T(8,128)(2,1)} fusion(bf16[32,16,10,2048]{3,2,0,1:T(8,128)(2,1)} %bitcast.78, f32[32,64,16]{1,2,0:T(8,128)S(1)} %get-tuple-element.12, f32[32,64,16]{1,2,0:T(8,128)S(1)} %copy.70), kind=kOutput, calls=%fused_computation.9 | convolution fusion | flops 1347026944 | bytes 29622272 | tf_op jit(solution)/shard_map/busr,bsrd->bud/dot_general | solution.py:116
  250.4 8.3 %copy.76 = bf16[8,4,64,2048]{3,2,0,1:T(8,128)(2,1)} copy(bf16[8,4,64,2048]{3,2,1,0:T(8,128)(2,1)} %bitcast.75) | data formatting | bytes 16777216 | tf_op jit(solution)/shard_map/reshape | solution.py:119
  258.7 70.5 %reduce-scatter.5.cloned.1.call-done = bf16[512,2048]{1,0:T(8,128)(2,1)} async-done(((bf16[2048,2048]{1,0:T(8,128)(2,1)}), bf16[512,2048]{1,0:T(8,128)(2,1)}) %reduce-scatter.5.cloned.1.call-update) | async-done | bytes 2097168 | tf_op jit(solution)/shard_map/reduce_scatter | solution.py:120
  329.2 53.7 %all_to_all.5 = bf16[8,64,2048]{2,1,0:T(8,128)(2,1)S(1)} all-to-all(bf16[8,64,2048]{2,1,0:T(8,128)(2,1)} %bitcast.81), channel_id=1, replica_groups=mesh['expert'=8,'tensor'=4] {'expert'}, dimensions={0} | all-to-all | bytes 4194304 | tf_op jit(solution)/shard_map/all_to_all | solution.py:126
  382.9 0.4 convert_reduce_fusion
  383.5 0.9 multiply_multiply_fusion
  (41 shorter events, 1.9 us)
Async XLA Ops:
  7.2 1.6 copy-start
  7.2 32.0 %reduce-scatter.3.cloned.1.call-start = ((), (), s32[]{:S(2)}) async-start(), calls=%async_computation.3 | async-start | bytes 1310720 | tf_op jit(solution)/shard_map/reduce_scatter | solution.py:52
  11.4 113.0 %all-gather.2.cloned.1.call-start = ((), (), s32[]{:S(2)}) async-start(), calls=%async_computation.4 | async-start | bytes 9191424 | tf_op jit(solution)/shard_map/all_gather | solution.py:70
  44.8 284.4 %reduce-scatter.5.cloned.1.call-start = ((), (), s32[]{:S(2)}) async-start(), calls=%async_computation.5 | async-start | bytes 10485760 | tf_op jit(solution)/shard_map/reduce_scatter | solution.py:120
  258.6 124.6 %copy-start.2 = (bf16[64,2048]{1,0:T(8,128)(2,1)S(1)}, bf16[64,2048]{1,0:T(8,128)(2,1)}, u32[]{:S(2)}) copy-start(bf16[64,2048]{1,0:T(8,128)(2,1)} %param.11) | copy-start | bytes 786436
  258.6 124.6 %copy-start.3 = (bf16[64,2048]{1,0:T(8,128)(2,1)S(1)}, bf16[64,2048]{1,0:T(8,128)(2,1)}, u32[]{:S(2)}) copy-start(bf16[64,2048]{1,0:T(8,128)(2,1)} %reduce-scatter.3.cloned.1.call-done) | copy-start | bytes 786436
  258.7 125.8 %copy-start.1 = (bf16[512,2048]{1,0:T(8,128)(2,1)S(1)}, bf16[512,2048]{1,0:T(8,128)(2,1)}, u32[]{:S(2)}) copy-start(bf16[512,2048]{1,0:T(8,128)(2,1)} %param.10) | copy-start | bytes 6291460
  258.7 124.9 %copy-start.5 = (f32[2048]{0:T(1024)S(1)}, f32[2048]{0:T(1024)}, u32[]{:S(2)}) copy-start(f32[2048]{0:T(1024)} %param.17) | copy-start | bytes 24580
  383.5 1.0 copy-start.4
Sparse Core Ops, SparseCore 0:
  11.6 27.5 reduce-scatter.2
  44.9 79.5 all-gather.1
  258.8 70.3 reduce-scatter.4

commit v9 on v8

--- a/solution.py
+++ b/solution.py
@@ -13,14 +13,14 @@
 
 def expert_inner(block_rows, weights):
     both_pre = jnp.einsum(
-        "nqsmd,scdf->nqsmcf", block_rows, weights[:, :2], preferred_element_type=jnp.float32
+        "sbmd,scdf->sbmcf", block_rows, weights[:, :2], preferred_element_type=jnp.float32
     )
     return jax.nn.silu(both_pre[..., 0, :]) * both_pre[..., 1, :]
 
 
 def expert_down(inner_act, weights):
     return jnp.einsum(
-        "nqsmf,sdf->nqsmd", inner_act, weights[:, 2], preferred_element_type=jnp.float32
+        "sbmf,sdf->sbmd", inner_act, weights[:, 2], preferred_element_type=jnp.float32
     )
 
 
@@ -103,18 +103,17 @@
     pick = token_hit[..., None] * (count_before[..., None] == rank_range)
     pick_hot = pick.astype(jnp.bfloat16)
     received = jnp.einsum(
-        "busr,bud->bsrd", pick_hot, all_rows, preferred_element_type=jnp.float32
-    ).astype(jnp.bfloat16).reshape(holders, groups, slot_dev, capacity, model_width)
+        "busr,bud->sbrd", pick_hot, all_rows, preferred_element_type=jnp.float32
+    ).astype(jnp.bfloat16)
     inner_f32 = expert_inner(received, expert_weights)
     if blocks * row_count * model_width * 4 <= (32 << 20):
         gate_sel = gate_sel_hi + gate_sel_lo
         pair_gate = jnp.sum(pick * gate_sel[..., None], axis=1)
-        pair_gate = pair_gate.reshape(holders, groups, slot_dev, capacity, 1)
+        pair_gate = jnp.swapaxes(pair_gate, 0, 1)[..., None]
         inner_act = (inner_f32 * pair_gate).astype(jnp.bfloat16)
         partial_value = expert_down(inner_act, expert_weights).astype(jnp.bfloat16)
-        partial_value = partial_value.reshape(blocks, slot_dev, capacity, model_width)
         combined = jnp.einsum(
-            "busr,bsrd->bud", pick_hot, partial_value, preferred_element_type=jnp.float32
+            "busr,sbrd->bud", pick_hot, partial_value, preferred_element_type=jnp.float32
         )
         token_sum = combined.astype(jnp.bfloat16).reshape(holders, groups, row_count, model_width)
         moe_sum = lax.psum_scatter(
@@ -129,6 +128,9 @@
         partial_value = expert_down(
             inner_f32.astype(jnp.bfloat16), expert_weights
         ).astype(jnp.bfloat16)
+        partial_value = jnp.transpose(
+            partial_value.reshape(slot_dev, holders, groups, capacity, model_width), (1, 2, 0, 3, 4)
+        )
         expert_sum = lax.psum_scatter(partial_value, "tensor", scatter_dimension=1, tiled=True)
         returned = lax.all_to_all(expert_sum, "expert", split_axis=0, concat_axis=0, tiled=True)
         own_flat = own_ids.reshape(-1)

time: 391 us -> 411 us (1.051)
  matrix products: 114 us -> 131 us
    dot_general x4, matrix products: 109 us -> 126 us  [the longest x1 49.3 us: on_device(): jnp.einsum('busr,sbrd->bud', pick_hot, partial_value, preferred_element_t...]
where the time goes in v9:
time: 411 us; the launch traced here: 410 us
  waiting for transfers between devices  175 us (43%)
  matrix products  131 us (32%)
  blocking collectives  53.7 us (13%)
  other arithmetic  22.4 us (5%)
  between operations  14.3 us (3%)
  local copies, waits for them, and re-layouts  12.7 us (3%)
    all_gather x1, waiting for transfers between devices, on_device(): lax.all_gather(jnp.concatenate([normed, side], axis=1), ('expert', 'tenso...  78.1 us
    reduce_scatter x1, waiting for transfers between devices, on_device(): lax.psum_scatter(jnp.swapaxes(token_sum, 0, 1).reshape(-1, model_width),...  70.5 us
    all_to_all x1, blocking collectives, on_device(): lax.all_to_all(moe_sum, 'expert', split_axis=0, concat_axis=0, tiled=True)  53.7 us
    dot_general x1, matrix products, on_device(): jnp.einsum('busr,sbrd->bud', pick_hot, partial_value, preferred_element_t...  49.3 us
    dot_general x1, matrix products, expert_inner(): jnp.einsum('sbmd,scdf->sbmcf', block_rows, weights[:, :2], preferred_elem...  41.1 us
    reduce_scatter x1, waiting for transfers between devices, on_device(): lax.psum_scatter(jnp.dot(context, out_proj, preferred_element_type=jnp.fl...  26.8 us
    dot_general x1, matrix products, expert_down(): jnp.einsum('sbmf,sdf->sbmd', inner_act, weights[:, 2], preferred_element_...  23.3 us
    dot_general x1, matrix products, on_device(): jnp.einsum('busr,bud->sbrd', pick_hot, all_rows, preferred_element_type=j...  12 us
  transfers between devices with their start and end apart: 3, of which 3 were waited for; matrix products, arithmetic and copies ran while one was open for 1% of the time, Pallas kernels for 0%

profile of v9, /device:TPU:0, one launch (start us, length us, event | category | flops | bytes accessed | tf_op | source)
XLA Modules:
  0.0 409.7 jit_solution(3504951598978570740)
XLA Ops:
  7.3 1.6 copy-done
  8.9 2.7 convolution_convert_fusion
  11.7 0.8 fusion.64
  12.5 26.8 %reduce-scatter.3.cloned.1.call-done = bf16[64,2048]{1,0:T(8,128)(2,1)} async-done(((bf16[256,2048]{1,0:T(8,128)(2,1)}), bf16[64,2048]{1,0:T(8,128)(2,1)}) %reduce-scatter.3.cloned.1.call-update) | async-done | bytes 262160 | tf_op jit(solution)/shard_map/reduce_scatter | solution.py:52
  39.3 1.2 multiply_reduce_fusion.1
  40.6 1.7 fusion.40
  42.3 0.2 select_reduce_fusion.1
  42.9 1.1 fusion.41
  43.9 0.7 fusion.42
  44.8 0.3 reduce_window_sum.11
  45.4 0.3 select_reduce_fusion
  45.8 0.6 gather_fusion
  46.4 78.1 %all-gather.2.cloned.1.call-done = bf16[2048,2176]{1,0:T(8,128)(2,1)} async-done(((bf16[64,2176]{1,0:T(8,128)(2,1)}), bf16[2048,2176]{1,0:T(8,128)(2,1)}) %all-gather.2.cloned.1.call-update) | async-done | bytes 8912912 | tf_op jit(solution)/shard_map/all_gather | solution.py:70
  124.5 2.1 fusion.65
  126.6 3.5 fusion.14
  130.2 1.0 copy.60
  131.2 8.1 %fusion.20 = (bf16[32,64,64]{2,1,0:T(8,128)(2,1)S(1)}, bf16[32,64,64]{2,1,0:T(8,128)(2,1)S(1)}) fusion(s32[32,64,8]{2,1,0:T(8,128)S(1)} %get-tuple-element.10, bf16[32,64,8]{2,1,0:T(8,128)(2,1)S(1)} %get-tuple-element.9, bf16[32,64,8]{2,1,0:T(8,128)(2,1)S(1)} %get-tuple-element.8), kind=kLoop, calls=%fused_computation.23 | loop fusion | flops 4980736 | bytes 655360 | tf_op jit(solution)/shard_map/reduce_sum | solution.py:90
  139.3 0.3 copy.61
  139.6 1.1 convert_element_type.86
  140.7 0.3 copy.62
  141.0 0.6 fusion.32
  142.1 12.0 %convert_bitcast_fusion = bf16[16,32,10,2048,1]{3,0,2,1,4:T(8,128)(2,1)} fusion(bf16[32,64,2176]{2,1,0:T(8,128)(2,1)} %bitcast.66, f32[32,64,16]{1,2,0:T(8,128)S(1)} %get-tuple-element.12, f32[32,64,16]{1,2,0:T(8,128)S(1)} %copy.64), kind=kOutput, calls=%fused_computation.7 | convolution fusion | flops 1353318400 | bytes 29622272 | tf_op jit(solution)/shard_map/busr,bud->sbrd/dot_general | solution.py:105
  154.2 0.8 fusion.22
  155.1 41.1 %fusion = f32[16,32,10,2,256]{4,1,3,2,0:T(8,128)} fusion(bf16[16,3,2048,256]{3,2,1,0:T(8,128)(2,1)} %param.16, bf16[16,32,10,2048,1]{3,0,2,1,4:T(8,128)(2,1)} %convert_bitcast_fusion), kind=kOutput, calls=%fused_computation.1 | convolution fusion | flops 10737418240 | bytes 65011712 | tf_op jit(solution)/shard_map/sbmd,scdf->sbmcf/dot_general | solution.py:15
  196.2 23.3 %fusion.9 = bf16[16,32,10,2048]{3,1,2,0:T(8,128)(2,1)} fusion(bf16[16,3,2048,256]{3,2,1,0:T(8,128)(2,1)} %param.16, f32[16,32,10,2,256]{4,1,3,2,0:T(8,128)} %fusion, f32[16,32,10]{1,2,0:T(8,128)S(1)} %copy.67), kind=kOutput, calls=%fused_computation.12 | convolution fusion | flops 5388369920 | bytes 48254976 | tf_op jit(solution)/shard_map/sbmf,sdf->sbmd/dot_general | solution.py:22
  219.5 49.3 %bitcast_convert_fusion = bf16[32,64,2048]{2,1,0:T(8,128)(2,1)} fusion(bf16[16,32,10,2048]{3,1,2,0:T(8,128)(2,1)} %fusion.9, f32[32,64,16]{1,2,0:T(8,128)S(1)} %get-tuple-element.12, f32[32,64,16]{1,2,0:T(8,128)S(1)} %copy.64), kind=kOutput, calls=%fused_computation.10 | convolution fusion | flops 1347026944 | bytes 29622272 | tf_op jit(solution)/shard_map/busr,sbrd->bud/dot_general | solution.py:115
  268.9 8.3 %copy.70 = bf16[8,4,64,2048]{3,2,0,1:T(8,128)(2,1)} copy(bf16[8,4,64,2048]{3,2,1,0:T(8,128)(2,1)} %bitcast.61) | data formatting | bytes 16777216 | tf_op jit(solution)/shard_map/reshape | solution.py:118
  277.2 70.5 %reduce-scatter.5.cloned.1.call-done = bf16[512,2048]{1,0:T(8,128)(2,1)} async-done(((bf16[2048,2048]{1,0:T(8,128)(2,1)}), bf16[512,2048]{1,0:T(8,128)(2,1)}) %reduce-scatter.5.cloned.1.call-update) | async-done | bytes 2097168 | tf_op jit(solution)/shard_map/reduce_scatter | solution.py:119
  347.6 53.7 %all_to_all.5 = bf16[8,64,2048]{2,1,0:T(8,128)(2,1)S(1)} all-to-all(bf16[8,64,2048]{2,1,0:T(8,128)(2,1)} %bitcast.63), channel_id=1, replica_groups=mesh['expert'=8,'tensor'=4] {'expert'}, dimensions={0} | all-to-all | bytes 4194304 | tf_op jit(solution)/shard_map/all_to_all | solution.py:125
  401.4 0.4 convert_reduce_fusion
  401.8 0.2 multiply_reduce_fusion
  402.0 0.9 multiply_multiply_fusion
  (47 shorter events, 1.7 us)
Async XLA Ops:
  7.2 1.8 copy-start
  7.2 35.7 %copy-start.2 = (bf16[64,2048]{1,0:T(8,128)(2,1)S(1)}, bf16[64,2048]{1,0:T(8,128)(2,1)}, u32[]{:S(2)}) copy-start(bf16[64,2048]{1,0:T(8,128)(2,1)} %param.11) | copy-start | bytes 786436
  7.2 35.7 %copy-start.6 = (f32[2048]{0:T(1024)S(1)}, f32[2048]{0:T(1024)}, u32[]{:S(2)}) copy-start(f32[2048]{0:T(1024)} %param.12) | copy-start | bytes 24580
  7.2 33.4 %copy-start.5 = (f32[2048,64]{0,1:T(8,128)S(1)}, f32[2048,64]{0,1:T(8,128)}, u32[]{:S(2)}) copy-start(f32[2048,64]{0,1:T(8,128)} %param.13) | copy-start | bytes 1572868
  7.2 37.5 %copy-start.8 = (s32[128]{0:T(128)S(1)}, s32[128]{0:T(128)}, u32[]{:S(2)}) copy-start(s32[128]{0:T(128)} %param.15) | copy-start | bytes 1540
  7.2 32.1 %reduce-scatter.3.cloned.1.call-start = ((), (), s32[]{:S(2)}) async-start(), calls=%async_computation.3 | async-start | bytes 1310720 | tf_op jit(solution)/shard_map/reduce_scatter | solution.py:52
  11.6 112.9 %all-gather.2.cloned.1.call-start = ((), (), s32[]{:S(2)}) async-start(), calls=%async_computation.4 | async-start | bytes 9191424 | tf_op jit(solution)/shard_map/all_gather | solution.py:70
  44.7 303.0 %reduce-scatter.5.cloned.1.call-start = ((), (), s32[]{:S(2)}) async-start(), calls=%async_computation.5 | async-start | bytes 10485760 | tf_op jit(solution)/shard_map/reduce_scatter | solution.py:119
  277.1 124.6 %copy-start.3 = (bf16[64,2048]{1,0:T(8,128)(2,1)S(1)}, bf16[64,2048]{1,0:T(8,128)(2,1)}, u32[]{:S(2)}) copy-start(bf16[64,2048]{1,0:T(8,128)(2,1)} %reduce-scatter.3.cloned.1.call-done) | copy-start | bytes 786436
  277.2 124.8 %copy-start.7 = (f32[2048]{0:T(1024)S(1)}, f32[2048]{0:T(1024)}, u32[]{:S(2)}) copy-start(f32[2048]{0:T(1024)} %param.17) | copy-start | bytes 24580
  277.2 125.8 %copy-start.1 = (bf16[512,2048]{1,0:T(8,128)(2,1)S(1)}, bf16[512,2048]{1,0:T(8,128)(2,1)}, u32[]{:S(2)}) copy-start(bf16[512,2048]{1,0:T(8,128)(2,1)} %param.10) | copy-start | bytes 6291460
  402.0 1.0 copy-start.4
Sparse Core Ops, SparseCore 0:
  11.7 27.5 reduce-scatter.2
  44.8 79.6 all-gather.1
  277.3 70.3 reduce-scatter.4

commit v10 on v8

--- a/solution.py
+++ b/solution.py
@@ -117,12 +117,10 @@
             "busr,bsrd->bud", pick_hot, partial_value, preferred_element_type=jnp.float32
         )
         token_sum = combined.astype(jnp.bfloat16).reshape(holders, groups, row_count, model_width)
-        moe_sum = lax.psum_scatter(
-            jnp.swapaxes(token_sum, 0, 1).reshape(-1, model_width),
-            "tensor",
-            scatter_dimension=0,
-            tiled=True,
-        ).reshape(holders, row_count, model_width)
+        moe_sum = lax.all_to_all(
+            jnp.swapaxes(token_sum, 0, 1), "tensor", split_axis=0, concat_axis=0, tiled=True
+        )
+        moe_sum = jnp.sum(moe_sum.astype(jnp.float32), axis=0).astype(jnp.bfloat16)
         moe_sum = lax.all_to_all(moe_sum, "expert", split_axis=0, concat_axis=0, tiled=True)
         moe_sum = jnp.sum(moe_sum.astype(jnp.float32), axis=0)
     else:

time: 391 us -> 428 us (1.095)
  blocking collectives: 53.7 us -> 153 us
  waiting for transfers between devices: 174 us -> 104 us
  other arithmetic: 22.8 us -> 30.1 us
    all_to_all x0 -> x1, blocking collectives: none -> 101 us  [on_device(): lax.all_to_all(jnp.swapaxes(token_sum, 0, 1), 'tensor', split_axis=0, con...]
    reduce_scatter x1 -> x0, waiting for transfers between devices: 70.5 us -> none  [on_device(): lax.psum_scatter(jnp.swapaxes(token_sum, 0, 1).reshape(-1, model_width),...]
    reduce_sum x0 -> x1, other arithmetic: none -> 7.25 us  [on_device(): moe_sum = jnp.sum(moe_sum.astype(jnp.float32), axis=0).astype(jnp.bfloat16)]
  transfers between devices with their start and end apart: 3 -> 2, of which waited for: 3 -> 2; matrix products, arithmetic and copies ran while one was open for 1% -> 1% of each run, Pallas kernels for 0% -> 0%
where the time goes in v10:
time: 428 us; the launch traced here: 427 us
  blocking collectives  153 us (36%)
  matrix products  114 us (27%)
  waiting for transfers between devices  104 us (24%)
  other arithmetic  30.1 us (7%)
  between operations  14.3 us (3%)
  local copies, waits for them, and re-layouts  12.2 us (3%)
    all_to_all x1, blocking collectives, on_device(): lax.all_to_all(jnp.swapaxes(token_sum, 0, 1), 'tensor', split_axis=0, con...  101 us
    all_gather x1, waiting for transfers between devices, on_device(): lax.all_gather(jnp.concatenate([normed, side], axis=1), ('expert', 'tenso...  76.8 us
    all_to_all x1, blocking collectives, on_device(): lax.all_to_all(moe_sum, 'expert', split_axis=0, concat_axis=0, tiled=True)  51.9 us
    dot_general x1, matrix products, expert_inner(): jnp.einsum('nqsmd,scdf->nqsmcf', block_rows, weights[:, :2], preferred_el...  46.3 us
    reduce_scatter x1, waiting for transfers between devices, on_device(): lax.psum_scatter(jnp.dot(context, out_proj, preferred_element_type=jnp.fl...  26.8 us
    dot_general x1, matrix products, on_device(): jnp.einsum('busr,bsrd->bud', pick_hot, partial_value, preferred_element_t...  25.6 us
    dot_general x1, matrix products, expert_down(): jnp.einsum('nqsmf,sdf->nqsmd', inner_act, weights[:, 2], preferred_elemen...  23.3 us
    dot_general x1, matrix products, on_device(): jnp.einsum('busr,bud->bsrd', pick_hot, all_rows, preferred_element_type=j...  13.4 us
  transfers between devices with their start and end apart: 2, of which 2 were waited for; matrix products, arithmetic and copies ran while one was open for 1% of the time, Pallas kernels for 0%

profile of v10, /device:TPU:0, one launch (start us, length us, event | category | flops | bytes accessed | tf_op | source)
XLA Modules:
  0.0 427.2 jit_solution(11627614255715820538)
XLA Ops:
  7.2 1.5 copy-done
  8.8 2.7 convolution_convert_fusion.2
  11.5 0.8 fusion.65
  12.3 26.8 %reduce-scatter.2.cloned.1.call-done = bf16[64,2048]{1,0:T(8,128)(2,1)} async-done(((bf16[256,2048]{1,0:T(8,128)(2,1)}), bf16[64,2048]{1,0:T(8,128)(2,1)}) %reduce-scatter.2.cloned.1.call-update) | async-done | bytes 262160 | tf_op jit(solution)/shard_map/reduce_scatter | solution.py:52
  39.2 1.2 multiply_reduce_fusion.1
  40.4 1.9 fusion.41
  42.9 1.2 fusion.42
  44.0 0.7 fusion.43
  44.8 0.7 fusion.51
  45.4 0.3 reduce_window_sum.11
  45.8 0.8 fusion.50
  46.7 0.3 select_reduce_fusion
  47.1 0.6 gather_fusion
  47.7 76.8 %all-gather.2.cloned.1.call-done = bf16[2048,2176]{1,0:T(8,128)(2,1)} async-done(((bf16[64,2176]{1,0:T(8,128)(2,1)}), bf16[2048,2176]{1,0:T(8,128)(2,1)}) %all-gather.2.cloned.1.call-update) | async-done | bytes 8912912 | tf_op jit(solution)/shard_map/all_gather | solution.py:70
  124.5 2.1 fusion.66
  126.6 3.5 fusion.18
  130.2 0.4 copy.65
  130.6 8.1 %fusion.21 = (bf16[32,64,64]{2,1,0:T(8,128)(2,1)S(1)}, bf16[32,64,64]{2,1,0:T(8,128)(2,1)S(1)}) fusion(s32[32,64,8]{2,1,0:T(8,128)S(1)} %get-tuple-element.10, bf16[32,64,8]{2,1,0:T(8,128)(2,1)S(1)} %get-tuple-element.9, bf16[32,64,8]{2,1,0:T(8,128)(2,1)S(1)} %get-tuple-element.8), kind=kLoop, calls=%fused_computation.24 | loop fusion | flops 4980736 | bytes 655360 | tf_op jit(solution)/shard_map/reduce_sum | solution.py:90
  139.1 0.3 copy.67
  139.4 0.6 fusion.33
  140.6 13.4 %convolution_convert_fusion.1 = bf16[32,16,10,2048]{3,1,2,0:T(8,128)(2,1)} fusion(bf16[32,64,2176]{2,1,0:T(8,128)(2,1)} %bitcast.79, f32[32,64,16]{1,2,0:T(8,128)S(1)} %get-tuple-element.12, f32[32,64,16]{1,2,0:T(8,128)S(1)} %copy.69), kind=kOutput, calls=%fused_computation.11 | convolution fusion | flops 1353318400 | bytes 29622272 | tf_op jit(solution)/shard_map/busr,bud->bsrd/dot_general | solution.py:105
  153.9 0.8 fusion.26
  154.7 0.4 copy.72
  155.1 46.3 %fusion.8 = f32[8,4,16,10,2,256]{5,3,4,1,0,2:T(8,128)} fusion(bf16[16,3,2048,256]{3,2,1,0:T(8,128)(2,1)} %param.16, bf16[8,4,16,10,2048,1]{4,2,3,1,0,5:T(8,128)(2,1)} %bitcast.75), kind=kOutput, calls=%fused_computation.12 | convolution fusion | flops 10737418240 | bytes 65011712 | tf_op jit(solution)/shard_map/nqsmd,scdf->nqsmcf/dot_general | solution.py:15
  201.4 23.3 %convolution_convert_fusion = bf16[16,8,4,10,2048]{4,3,2,1,0:T(8,128)(2,1)} fusion(bf16[16,3,2048,256]{3,2,1,0:T(8,128)(2,1)} %param.16, f32[8,4,16,10,2,256]{5,3,4,1,0,2:T(8,128)} %fusion.8, f32[8,4,16,10]{3,1,0,2:T(4,128)S(1)} %copy.72), kind=kOutput, calls=%fused_computation.7 | convolution fusion | flops 5388369920 | bytes 54546432 | tf_op jit(solution)/shard_map/nqsmf,sdf->nqsmd/dot_general | solution.py:22
  224.7 25.6 %bitcast_convert_fusion = bf16[32,64,2048]{2,1,0:T(8,128)(2,1)} fusion(bf16[32,16,10,2048]{3,2,0,1:T(8,128)(2,1)} %bitcast.77, f32[32,64,16]{1,2,0:T(8,128)S(1)} %get-tuple-element.12, f32[32,64,16]{1,2,0:T(8,128)S(1)} %copy.69), kind=kOutput, calls=%fused_computation.9 | convolution fusion | flops 1347026944 | bytes 29622272 | tf_op jit(solution)/shard_map/busr,bsrd->bud/dot_general | solution.py:116
  250.4 8.3 %copy.97 = bf16[8,4,64,2048]{3,2,0,1:T(8,128)(2,1)} copy(bf16[8,4,64,2048]{3,2,1,0:T(8,128)(2,1)} %bitcast.74) | data formatting | bytes 16777216 | tf_op jit(solution)/shard_map/reshape | solution.py:119
  258.6 101.0 %all_to_all.10 = bf16[4,8,64,2048]{3,2,1,0:T(8,128)(2,1)} all-to-all(bf16[4,8,64,2048]{3,2,1,0:T(8,128)(2,1)} %bitcast.76), channel_id=1, replica_groups=mesh['expert'=8,'tensor'=4] {'tensor'}, dimensions={0} | all-to-all | bytes 16777216 | tf_op jit(solution)/shard_map/all_to_all | solution.py:120
  359.7 7.2 %reduce_sum.116 = bf16[8,64,2048]{2,1,0:T(8,128)(2,1)} reduce(bf16[4,8,64,2048]{3,2,1,0:T(8,128)(2,1)} %all_to_all.10, bf16[]{:T(256)} %constant.60.clone.1), dimensions={0}, to_apply=%region_12.13 | reduce | flops 3145728 | bytes 10485762 | tf_op jit(solution)/shard_map/reduce_sum | solution.py:123
  366.9 51.9 %all_to_all.11 = bf16[8,64,2048]{2,1,0:T(8,128)(2,1)S(1)} all-to-all(bf16[8,64,2048]{2,1,0:T(8,128)(2,1)} %reduce_sum.116), channel_id=1, replica_groups=mesh['expert'=8,'tensor'=4] {'expert'}, dimensions={0} | all-to-all | bytes 4194304 | tf_op jit(solution)/shard_map/all_to_all | solution.py:124
  418.8 0.4 convert_reduce_fusion
  419.4 0.9 multiply_multiply_fusion
  (40 shorter events, 2.1 us)
Async XLA Ops:
  7.2 1.6 copy-start
  7.2 32.0 %reduce-scatter.2.cloned.1.call-start = ((), (), s32[]{:S(2)}) async-start(), calls=%async_computation.3 | async-start | bytes 1310720 | tf_op jit(solution)/shard_map/reduce_scatter | solution.py:52
  11.4 113.0 %all-gather.2.cloned.1.call-start = ((), (), s32[]{:S(2)}) async-start(), calls=%async_computation.4 | async-start | bytes 9191424 | tf_op jit(solution)/shard_map/all_gather | solution.py:70
  258.6 161.7 %copy-start.1 = (bf16[512,2048]{1,0:T(8,128)(2,1)S(1)}, bf16[512,2048]{1,0:T(8,128)(2,1)}, u32[]{:S(2)}) copy-start(bf16[512,2048]{1,0:T(8,128)(2,1)} %param.10) | copy-start | bytes 6291460
  359.7 59.5 %copy-start.2 = (bf16[64,2048]{1,0:T(8,128)(2,1)S(1)}, bf16[64,2048]{1,0:T(8,128)(2,1)}, u32[]{:S(2)}) copy-start(bf16[64,2048]{1,0:T(8,128)(2,1)} %param.11) | copy-start | bytes 786436
  359.7 59.5 %copy-start.3 = (bf16[64,2048]{1,0:T(8,128)(2,1)S(1)}, bf16[64,2048]{1,0:T(8,128)(2,1)}, u32[]{:S(2)}) copy-start(bf16[64,2048]{1,0:T(8,128)(2,1)} %reduce-scatter.2.cloned.1.call-done) | copy-start | bytes 786436
  359.7 59.7 %copy-start.5 = (f32[2048]{0:T(1024)S(1)}, f32[2048]{0:T(1024)}, u32[]{:S(2)}) copy-start(f32[2048]{0:T(1024)} %param.17) | copy-start | bytes 24580
  419.4 1.0 copy-start.4
Sparse Core Ops, SparseCore 0:
  11.6 27.5 reduce-scatter.1
  44.9 79.5 all-gather.1

commit v11 on v8

--- a/solution.py
+++ b/solution.py
@@ -49,12 +49,16 @@
     capacity = max(2, row_count * top_count * 5 // (expert_count * 4))
     expert_range = jnp.arange(expert_count, dtype=jnp.int32)
     slot_range = jnp.arange(slot_total, dtype=jnp.int32)
-    attention = lax.psum_scatter(
-        jnp.dot(context, out_proj, preferred_element_type=jnp.float32).astype(jnp.bfloat16),
+    attention_parts = lax.all_to_all(
+        jnp.dot(context, out_proj, preferred_element_type=jnp.float32)
+        .astype(jnp.bfloat16)
+        .reshape(groups, row_count, -1),
         "tensor",
-        scatter_dimension=0,
+        split_axis=0,
+        concat_axis=0,
         tiled=True,
-    ).astype(jnp.float32)
+    )
+    attention = jnp.sum(attention_parts.astype(jnp.float32), axis=0)
     hidden_mid = residual.astype(jnp.float32) + attention
     normed_full = rms_scale(hidden_mid, norm_gain)
     normed = normed_full.astype(jnp.bfloat16)

time: 391 us -> 388 us (level)
  waiting for transfers between devices: 174 us -> 163 us
  starting transfers between devices: 0.12 us -> 4.28 us
    reduce_scatter x1 -> x0, waiting for transfers between devices: 26.8 us -> none  [on_device(): lax.psum_scatter(jnp.dot(context, out_proj, preferred_element_type=jnp.fl...]
    all_to_all x0 -> x1, waiting for transfers between devices: none -> 13.6 us  [on_device(): lax.all_to_all(jnp.dot(context, out_proj, preferred_element_type=jnp.floa...]
    all_to_all x0 -> x1, starting transfers between devices: none -> 4.24 us  [on_device(): lax.all_to_all(jnp.dot(context, out_proj, preferred_element_type=jnp.floa...]
where the time goes in v11:
time: 388 us; the launch traced here: 387 us
  waiting for transfers between devices  163 us (42%)
  matrix products  114 us (29%)
  blocking collectives  53.7 us (14%)
  other arithmetic  23.2 us (6%)
  local copies, waits for them, and re-layouts  14.6 us (4%)
  between operations  14.3 us (4%)
  starting transfers between devices  4.28 us (1%)
    all_gather x1, waiting for transfers between devices, on_device(): lax.all_gather(jnp.concatenate([normed, side], axis=1), ('expert', 'tenso...  79.1 us
    reduce_scatter x1, waiting for transfers between devices, on_device(): lax.psum_scatter(jnp.swapaxes(token_sum, 0, 1).reshape(-1, model_width),...  70.5 us
    all_to_all x1, blocking collectives, on_device(): lax.all_to_all(moe_sum, 'expert', split_axis=0, concat_axis=0, tiled=True)  53.7 us
    dot_general x1, matrix products, expert_inner(): jnp.einsum('nqsmd,scdf->nqsmcf', block_rows, weights[:, :2], preferred_el...  46.3 us
    dot_general x1, matrix products, on_device(): jnp.einsum('busr,bsrd->bud', pick_hot, partial_value, preferred_element_t...  25.6 us
    dot_general x1, matrix products, expert_down(): jnp.einsum('nqsmf,sdf->nqsmd', inner_act, weights[:, 2], preferred_elemen...  23.3 us
    all_to_all x1, waiting for transfers between devices, on_device(): lax.all_to_all(jnp.dot(context, out_proj, preferred_element_type=jnp.floa...  13.6 us
    dot_general x1, matrix products, on_device(): jnp.einsum('busr,bud->bsrd', pick_hot, all_rows, preferred_element_type=j...  13.4 us
  transfers between devices with their start and end apart: 3, of which 3 were waited for; matrix products, arithmetic and copies ran while one was open for 1% of the time, Pallas kernels for 0%

profile of v11, /device:TPU:0, one launch (start us, length us, event | category | flops | bytes accessed | tf_op | source)
XLA Modules:
  0.0 387.2 jit_solution(15570589036099552011)
XLA Ops:
  7.2 1.5 copy-done
  8.8 2.7 convolution_convert_fusion.2
  11.4 4.2 %all-to-all-start = ((bf16[4,64,2048]{2,1,0:T(8,128)(2,1)}), bf16[4,64,2048]{2,1,0:T(8,128)(2,1)S(1)}, u32[]{:S(2)}, u32[]{:S(2)}) async-start(bf16[4,64,2048]{2,1,0:T(8,128)(2,1)} %bitcast), calls=%async_computation | async-start | bytes 2097152 | tf_op jit(solution)/shard_map/all_to_all | solution.py:52
  15.7 0.8 fusion.65
  16.5 13.6 %all-to-all-done = bf16[4,64,2048]{2,1,0:T(8,128)(2,1)S(1)} async-done(((bf16[4,64,2048]{2,1,0:T(8,128)(2,1)}), bf16[4,64,2048]{2,1,0:T(8,128)(2,1)S(1)}, u32[]{:S(2)}, u32[]{:S(2)}) %all-to-all-start) | async-done | bytes 1048608 | tf_op jit(solution)/shard_map/all_to_all | solution.py:52
  30.3 1.1 multiply_reduce_fusion.1
  31.4 1.1 fusion.41
  32.5 0.6 fusion.40
  33.8 0.7 fusion.42
  34.6 0.3 reduce_window_sum.11
  35.2 0.3 select_reduce_fusion
  35.6 0.6 gather_fusion
  36.2 79.1 %all-gather.2.cloned.1.call-done = bf16[2048,2176]{1,0:T(8,128)(2,1)} async-done(((bf16[64,2176]{1,0:T(8,128)(2,1)}), bf16[2048,2176]{1,0:T(8,128)(2,1)}) %all-gather.2.cloned.1.call-update) | async-done | bytes 8912912 | tf_op jit(solution)/shard_map/all_gather | solution.py:74
  115.3 2.1 fusion.66
  117.5 3.5 fusion.18
  121.0 1.0 copy.54
  122.1 8.8 %fusion.21 = (bf16[32,64,64]{2,1,0:T(8,128)(2,1)}, bf16[32,64,64]{2,1,0:T(8,128)(2,1)S(1)}) fusion(s32[32,64,8]{2,1,0:T(8,128)S(1)} %get-tuple-element.10, bf16[32,64,8]{2,1,0:T(8,128)(2,1)S(1)} %get-tuple-element.9, bf16[32,64,8]{2,1,0:T(8,128)(2,1)S(1)} %get-tuple-element.8), kind=kLoop, calls=%fused_computation.23 | loop fusion | flops 4980736 | bytes 655360 | tf_op jit(solution)/shard_map/reduce_sum | solution.py:94
  130.9 1.3 copy.55
  132.2 1.1 convert_element_type.86
  133.3 1.0 copy.56
  134.3 1.7 fusion.33
  136.5 13.4 %convolution_convert_fusion.1 = bf16[32,16,10,2048]{3,1,2,0:T(8,128)(2,1)} fusion(bf16[32,64,2176]{2,1,0:T(8,128)(2,1)} %bitcast.81, f32[32,64,16]{1,2,0:T(8,128)S(1)} %get-tuple-element.12, f32[32,64,16]{1,2,0:T(8,128)S(1)} %copy.58), kind=kOutput, calls=%fused_computation.11 | convolution fusion | flops 1353318400 | bytes 29622272 | tf_op jit(solution)/shard_map/busr,bud->bsrd/dot_general | solution.py:109
  149.9 0.8 fusion.26
  150.6 0.4 copy.61
  151.0 46.3 %fusion.8 = f32[8,4,16,10,2,256]{5,3,4,1,0,2:T(8,128)} fusion(bf16[16,3,2048,256]{3,2,1,0:T(8,128)(2,1)} %param.16, bf16[8,4,16,10,2048,1]{4,2,3,1,0,5:T(8,128)(2,1)} %bitcast.77), kind=kOutput, calls=%fused_computation.12 | convolution fusion | flops 10737418240 | bytes 65011712 | tf_op jit(solution)/shard_map/nqsmd,scdf->nqsmcf/dot_general | solution.py:15
  197.3 23.3 %convolution_convert_fusion = bf16[16,8,4,10,2048]{4,3,2,1,0:T(8,128)(2,1)} fusion(bf16[16,3,2048,256]{3,2,1,0:T(8,128)(2,1)} %param.16, f32[8,4,16,10,2,256]{5,3,4,1,0,2:T(8,128)} %fusion.8, f32[8,4,16,10]{3,1,0,2:T(4,128)S(1)} %copy.61), kind=kOutput, calls=%fused_computation.7 | convolution fusion | flops 5388369920 | bytes 54546432 | tf_op jit(solution)/shard_map/nqsmf,sdf->nqsmd/dot_general | solution.py:22
  220.7 25.6 %bitcast_convert_fusion = bf16[32,64,2048]{2,1,0:T(8,128)(2,1)} fusion(bf16[32,16,10,2048]{3,2,0,1:T(8,128)(2,1)} %bitcast.79, f32[32,64,16]{1,2,0:T(8,128)S(1)} %get-tuple-element.12, f32[32,64,16]{1,2,0:T(8,128)S(1)} %copy.58), kind=kOutput, calls=%fused_computation.9 | convolution fusion | flops 1347026944 | bytes 29622272 | tf_op jit(solution)/shard_map/busr,bsrd->bud/dot_general | solution.py:120
  246.3 8.3 %copy.64 = bf16[8,4,64,2048]{3,2,0,1:T(8,128)(2,1)} copy(bf16[8,4,64,2048]{3,2,1,0:T(8,128)(2,1)} %bitcast.76) | data formatting | bytes 16777216 | tf_op jit(solution)/shard_map/reshape | solution.py:123
  254.6 70.5 %reduce-scatter.2.cloned.1.call-done = bf16[512,2048]{1,0:T(8,128)(2,1)} async-done(((bf16[2048,2048]{1,0:T(8,128)(2,1)}), bf16[512,2048]{1,0:T(8,128)(2,1)}) %reduce-scatter.2.cloned.1.call-update) | async-done | bytes 2097168 | tf_op jit(solution)/shard_map/reduce_scatter | solution.py:124
  325.1 53.7 %all_to_all.10 = bf16[8,64,2048]{2,1,0:T(8,128)(2,1)S(1)} all-to-all(bf16[8,64,2048]{2,1,0:T(8,128)(2,1)} %bitcast.82), channel_id=1, replica_groups=mesh['expert'=8,'tensor'=4] {'expert'}, dimensions={0} | all-to-all | bytes 4194304 | tf_op jit(solution)/shard_map/all_to_all | solution.py:130
  378.9 0.4 convert_reduce_fusion
  379.4 0.9 multiply_multiply_fusion
  (45 shorter events, 2.0 us)
Async XLA Ops:
  7.2 1.6 copy-start
  7.2 25.3 %copy-start.2 = (bf16[64,2048]{1,0:T(8,128)(2,1)S(1)}, bf16[64,2048]{1,0:T(8,128)(2,1)}, u32[]{:S(2)}) copy-start(bf16[64,2048]{1,0:T(8,128)(2,1)} %param.11) | copy-start | bytes 786436
  7.2 25.3 %copy-start.5 = (f32[2048]{0:T(1024)S(1)}, f32[2048]{0:T(1024)}, u32[]{:S(2)}) copy-start(f32[2048]{0:T(1024)} %param.12) | copy-start | bytes 24580
  7.2 25.3 %copy-start.4 = (f32[2048,64]{0,1:T(8,128)S(1)}, f32[2048,64]{0,1:T(8,128)}, u32[]{:S(2)}) copy-start(f32[2048,64]{0,1:T(8,128)} %param.13) | copy-start | bytes 1572868
  7.2 27.4 %copy-start.7 = (s32[128]{0:T(128)S(1)}, s32[128]{0:T(128)}, u32[]{:S(2)}) copy-start(s32[128]{0:T(128)} %param.15) | copy-start | bytes 1540
  11.4 18.7 %all-to-all-start = ((bf16[4,64,2048]{2,1,0:T(8,128)(2,1)}), bf16[4,64,2048]{2,1,0:T(8,128)(2,1)S(1)}, u32[]{:S(2)}, u32[]{:S(2)}) async-start(bf16[4,64,2048]{2,1,0:T(8,128)(2,1)} %bitcast), calls=%async_computation | async-start | bytes 2097152 | tf_op jit(solution)/shard_map/all_to_all | solution.py:52
  15.7 99.7 %all-gather.2.cloned.1.call-start = ((), (), s32[]{:S(2)}) async-start(), calls=%async_computation.3 | async-start | bytes 9191424 | tf_op jit(solution)/shard_map/all_gather | solution.py:74
  34.5 290.6 %reduce-scatter.2.cloned.1.call-start = ((), (), s32[]{:S(2)}) async-start(), calls=%async_computation.4 | async-start | bytes 10485760 | tf_op jit(solution)/shard_map/reduce_scatter | solution.py:124
  254.6 125.8 %copy-start.1 = (bf16[512,2048]{1,0:T(8,128)(2,1)S(1)}, bf16[512,2048]{1,0:T(8,128)(2,1)}, u32[]{:S(2)}) copy-start(bf16[512,2048]{1,0:T(8,128)(2,1)} %param.10) | copy-start | bytes 6291460
  254.6 124.9 %copy-start.6 = (f32[2048]{0:T(1024)S(1)}, f32[2048]{0:T(1024)}, u32[]{:S(2)}) copy-start(f32[2048]{0:T(1024)} %param.17) | copy-start | bytes 24580
  379.4 1.0 copy-start.3
Sparse Core Ops, SparseCore 0:
  34.7 80.6 all-gather.1
  254.7 70.3 reduce-scatter.1

commit v12 on v11

--- a/solution.py
+++ b/solution.py
@@ -118,11 +118,13 @@
         partial_value = expert_down(inner_act, expert_weights).astype(jnp.bfloat16)
         partial_value = partial_value.reshape(blocks, slot_dev, capacity, model_width)
         combined = jnp.einsum(
-            "busr,bsrd->bud", pick_hot, partial_value, preferred_element_type=jnp.float32
+            "hqusr,hqsrd->qhud",
+            pick_hot.reshape(holders, groups, row_count, slot_dev, capacity),
+            partial_value.reshape(holders, groups, slot_dev, capacity, model_width),
+            preferred_element_type=jnp.float32,
         )
-        token_sum = combined.astype(jnp.bfloat16).reshape(holders, groups, row_count, model_width)
         moe_sum = lax.psum_scatter(
-            jnp.swapaxes(token_sum, 0, 1).reshape(-1, model_width),
+            combined.astype(jnp.bfloat16).reshape(-1, model_width),
             "tensor",
             scatter_dimension=0,
             tiled=True,

time: 388 us -> 381 us (0.982)
  local copies, waits for them, and re-layouts: 14.6 us -> 6.49 us
    reshape x1 -> x0, local copies, waits for them, and re-layouts: 8.26 us -> none  [on_device(): combined.astype(jnp.bfloat16)]
where the time goes in v12:
time: 381 us
  waiting for transfers between devices  163 us (43%)
  matrix products  116 us (30%)
  blocking collectives  53.7 us (14%)
  other arithmetic  23.2 us (6%)
  between operations  14.3 us (4%)
  local copies, waits for them, and re-layouts  6.49 us (2%)
  starting transfers between devices  4.28 us (1%)
    all_gather x1, waiting for transfers between devices, on_device(): lax.all_gather(jnp.concatenate([normed, side], axis=1), ('expert', 'tenso...  79.1 us
    reduce_scatter x1, waiting for transfers between devices, on_device(): lax.psum_scatter(combined.astype(jnp.bfloat16).reshape(-1, model_width),...  70.5 us
    all_to_all x1, blocking collectives, on_device(): lax.all_to_all(moe_sum, 'expert', split_axis=0, concat_axis=0, tiled=True)  53.7 us
    dot_general x1, matrix products, expert_inner(): jnp.einsum('nqsmd,scdf->nqsmcf', block_rows, weights[:, :2], preferred_el...  46.3 us
    dot_general x1, matrix products, on_device(): jnp.einsum('hqusr,hqsrd->qhud', pick_hot.reshape(holders, groups, row_cou...  27.4 us
    dot_general x1, matrix products, expert_down(): jnp.einsum('nqsmf,sdf->nqsmd', inner_act, weights[:, 2], preferred_elemen...  23.3 us
    all_to_all x1, waiting for transfers between devices, on_device(): lax.all_to_all(jnp.dot(context, out_proj, preferred_element_type=jnp.floa...  13.6 us
    dot_general x1, matrix products, on_device(): jnp.einsum('busr,bud->bsrd', pick_hot, all_rows, preferred_element_type=j...  13.4 us
  transfers between devices with their start and end apart: 3, of which 3 were waited for; matrix products, arithmetic and copies ran while one was open for 1% of the time, Pallas kernels for 0%

profile of v12, /device:TPU:0, one launch (start us, length us, event | category | flops | bytes accessed | tf_op | source)
XLA Modules:
  0.0 380.9 jit_solution(10148748740071930744)
XLA Ops:
  7.2 1.5 copy-done
  8.8 2.7 convolution_convert_fusion.1
  11.4 4.2 %all-to-all-start = ((bf16[4,64,2048]{2,1,0:T(8,128)(2,1)}), bf16[4,64,2048]{2,1,0:T(8,128)(2,1)S(1)}, u32[]{:S(2)}, u32[]{:S(2)}) async-start(bf16[4,64,2048]{2,1,0:T(8,128)(2,1)} %bitcast), calls=%async_computation | async-start | bytes 2097152 | tf_op jit(solution)/shard_map/all_to_all | solution.py:52
  15.7 0.8 fusion.66
  16.5 13.6 %all-to-all-done = bf16[4,64,2048]{2,1,0:T(8,128)(2,1)S(1)} async-done(((bf16[4,64,2048]{2,1,0:T(8,128)(2,1)}), bf16[4,64,2048]{2,1,0:T(8,128)(2,1)S(1)}, u32[]{:S(2)}, u32[]{:S(2)}) %all-to-all-start) | async-done | bytes 1048608 | tf_op jit(solution)/shard_map/all_to_all | solution.py:52
  30.3 1.1 multiply_reduce_fusion.1
  31.4 1.1 fusion.41
  32.5 0.6 fusion.40
  33.2 0.2 select_reduce_fusion.1
  33.8 0.7 fusion.42
  34.6 0.3 reduce_window_sum.11
  35.2 0.3 select_reduce_fusion
  35.6 0.6 gather_fusion
  36.2 79.1 %all-gather.2.cloned.1.call-done = bf16[2048,2176]{1,0:T(8,128)(2,1)} async-done(((bf16[64,2176]{1,0:T(8,128)(2,1)}), bf16[2048,2176]{1,0:T(8,128)(2,1)}) %all-gather.2.cloned.1.call-update) | async-done | bytes 8912912 | tf_op jit(solution)/shard_map/all_gather | solution.py:74
  115.3 2.1 fusion.67
  117.5 3.5 fusion.18
  121.0 1.0 copy.55
  122.1 8.8 %fusion.21 = (bf16[32,64,64]{2,1,0:T(8,128)(2,1)}, bf16[32,64,64]{2,1,0:T(8,128)(2,1)S(1)}) fusion(s32[32,64,8]{2,1,0:T(8,128)S(1)} %get-tuple-element.10, bf16[32,64,8]{2,1,0:T(8,128)(2,1)S(1)} %get-tuple-element.9, bf16[32,64,8]{2,1,0:T(8,128)(2,1)S(1)} %get-tuple-element.8), kind=kLoop, calls=%fused_computation.23 | loop fusion | flops 4980736 | bytes 655360 | tf_op jit(solution)/shard_map/reduce_sum | solution.py:94
  130.9 1.3 copy.56
  132.2 1.1 convert_element_type.89
  133.3 1.0 copy.57
  134.3 1.7 fusion.33
  136.5 13.4 %convolution_convert_fusion = bf16[32,16,10,2048]{3,1,2,0:T(8,128)(2,1)} fusion(bf16[32,64,2176]{2,1,0:T(8,128)(2,1)} %bitcast.79, f32[32,64,16]{1,2,0:T(8,128)S(1)} %get-tuple-element.12, f32[32,64,16]{1,2,0:T(8,128)S(1)} %copy.61), kind=kOutput, calls=%fused_computation.11 | convolution fusion | flops 1353318400 | bytes 29622272 | tf_op jit(solution)/shard_map/busr,bud->bsrd/dot_general | solution.py:109
  149.9 0.8 fusion.26
  150.6 0.4 copy.64
  151.2 46.3 %fusion.8 = f32[8,4,16,10,2,256]{5,3,4,1,0,2:T(8,128)} fusion(bf16[16,3,2048,256]{3,2,1,0:T(8,128)(2,1)} %param.16, bf16[8,4,16,10,2048,1]{4,2,3,1,0,5:T(8,128)(2,1)} %bitcast.76), kind=kOutput, calls=%fused_computation.12 | convolution fusion | flops 10737418240 | bytes 65011712 | tf_op jit(solution)/shard_map/nqsmd,scdf->nqsmcf/dot_general | solution.py:15
  197.5 23.3 %convert_bitcast_fusion = bf16[8,4,16,10,2048]{4,3,1,0,2:T(8,128)(2,1)} fusion(bf16[16,3,2048,256]{3,2,1,0:T(8,128)(2,1)} %param.16, f32[8,4,16,10,2,256]{5,3,4,1,0,2:T(8,128)} %fusion.8, f32[8,4,16,10]{3,1,0,2:T(4,128)S(1)} %copy.64), kind=kOutput, calls=%fused_computation.4 | convolution fusion | flops 5388369920 | bytes 54546432 | tf_op jit(solution)/shard_map/nqsmf,sdf->nqsmd/dot_general | solution.py:22
  220.8 27.4 %bitcast_convert_fusion = bf16[4,8,64,2048]{3,2,1,0:T(8,128)(2,1)} fusion(bf16[8,4,16,10,2048]{4,3,1,0,2:T(8,128)(2,1)} %convert_bitcast_fusion, f32[8,4,64,16]{2,3,0,1:T(8,128)S(1)} %copy.59, f32[8,4,64,16]{2,3,1,0:T(8,128)S(1)} %bitcast.80), kind=kOutput, calls=%fused_computation.9 | convolution fusion | flops 1347026944 | bytes 29622272 | tf_op jit(solution)/shard_map/hqusr,hqsrd->qhud/dot_general | solution.py:120
  248.3 70.5 %reduce-scatter.2.cloned.1.call-done = bf16[512,2048]{1,0:T(8,128)(2,1)} async-done(((bf16[2048,2048]{1,0:T(8,128)(2,1)}), bf16[512,2048]{1,0:T(8,128)(2,1)}) %reduce-scatter.2.cloned.1.call-update) | async-done | bytes 2097168 | tf_op jit(solution)/shard_map/reduce_scatter | solution.py:126
  318.8 53.7 %all_to_all.10 = bf16[8,64,2048]{2,1,0:T(8,128)(2,1)S(1)} all-to-all(bf16[8,64,2048]{2,1,0:T(8,128)(2,1)} %bitcast.83), channel_id=1, replica_groups=mesh['expert'=8,'tensor'=4] {'expert'}, dimensions={0} | all-to-all | bytes 4194304 | tf_op jit(solution)/shard_map/all_to_all | solution.py:132
  372.5 0.4 convert_reduce_fusion
  373.1 0.9 multiply_multiply_fusion
  (45 shorter events, 1.9 us)
Async XLA Ops:
  7.2 1.6 copy-start
  7.2 25.3 %copy-start.2 = (bf16[64,2048]{1,0:T(8,128)(2,1)S(1)}, bf16[64,2048]{1,0:T(8,128)(2,1)}, u32[]{:S(2)}) copy-start(bf16[64,2048]{1,0:T(8,128)(2,1)} %param.11) | copy-start | bytes 786436
  7.2 25.3 %copy-start.5 = (f32[2048]{0:T(1024)S(1)}, f32[2048]{0:T(1024)}, u32[]{:S(2)}) copy-start(f32[2048]{0:T(1024)} %param.12) | copy-start | bytes 24580
  7.2 25.3 %copy-start.4 = (f32[2048,64]{0,1:T(8,128)S(1)}, f32[2048,64]{0,1:T(8,128)}, u32[]{:S(2)}) copy-start(f32[2048,64]{0,1:T(8,128)} %param.13) | copy-start | bytes 1572868
  7.2 27.4 %copy-start.7 = (s32[128]{0:T(128)S(1)}, s32[128]{0:T(128)}, u32[]{:S(2)}) copy-start(s32[128]{0:T(128)} %param.15) | copy-start | bytes 1540
  11.4 18.7 %all-to-all-start = ((bf16[4,64,2048]{2,1,0:T(8,128)(2,1)}), bf16[4,64,2048]{2,1,0:T(8,128)(2,1)S(1)}, u32[]{:S(2)}, u32[]{:S(2)}) async-start(bf16[4,64,2048]{2,1,0:T(8,128)(2,1)} %bitcast), calls=%async_computation | async-start | bytes 2097152 | tf_op jit(solution)/shard_map/all_to_all | solution.py:52
  15.7 99.7 %all-gather.2.cloned.1.call-start = ((), (), s32[]{:S(2)}) async-start(), calls=%async_computation.3 | async-start | bytes 9191424 | tf_op jit(solution)/shard_map/all_gather | solution.py:74
  34.5 284.3 %reduce-scatter.2.cloned.1.call-start = ((), (), s32[]{:S(2)}) async-start(), calls=%async_computation.4 | async-start | bytes 10485760 | tf_op jit(solution)/shard_map/reduce_scatter | solution.py:126
  248.2 125.8 %copy-start.1 = (bf16[512,2048]{1,0:T(8,128)(2,1)S(1)}, bf16[512,2048]{1,0:T(8,128)(2,1)}, u32[]{:S(2)}) copy-start(bf16[512,2048]{1,0:T(8,128)(2,1)} %param.10) | copy-start | bytes 6291460
  248.3 124.9 %copy-start.6 = (f32[2048]{0:T(1024)S(1)}, f32[2048]{0:T(1024)}, u32[]{:S(2)}) copy-start(f32[2048]{0:T(1024)} %param.17) | copy-start | bytes 24580
  373.1 1.0 copy-start.3
Sparse Core Ops, SparseCore 0:
  34.6 80.6 all-gather.1
  248.4 70.3 reduce-scatter.1
